TPU v7x, 128 devices: a whole 4x4x4 slice. The times are simulated.
128 devices in a mesh: expert: 32 (over y, z, core), dp: 4 (over x).
Axes of the slice: x: 4, y: 4, z: 4, core: 2. Of those that a mesh axis runs over, the one named last changes fastest.
Arguments:
- activations: bfloat16 [2048, 7168], P(('expert', 'dp')), may hold values from -6 to 6
- cotangent: bfloat16 [2048, 7168], P(('expert', 'dp')), may hold values from -6 to 6
- route_ids: int32 [2048, 8], P(('expert', 'dp')), may hold values from 0 to 31, all different within a row; in each aligned block of 16 rows (0 to 15, 16 to 31, ...) at most 5 rows name the same one
- route_weights: float32 [2048, 8], P(('expert', 'dp')), may hold values from 0.05 to 0.6
- gate_weights: bfloat16 [32, 7168, 1024], P('expert', 'dp'), may hold values from -0.0625 to 0.0625
- up_weights: bfloat16 [32, 7168, 1024], P('expert', 'dp'), may hold values from -0.0625 to 0.0625
- down_weights: bfloat16 [32, 1024, 7168], P('expert', None, 'dp'), may hold values from -0.1875 to 0.1875
Outputs:
- grad_input: bfloat16 [2048, 7168], P(('expert', 'dp'))
- grad_gate: bfloat16 [32, 7168, 1024], P('expert', 'dp')
- grad_up: bfloat16 [32, 7168, 1024], P('expert', 'dp')
- grad_down: bfloat16 [32, 1024, 7168], P('expert', None, 'dp')
Inputs may be any that keep to these rules, and one draw needn't show every extreme that they name: `route_ids`: each token names 8 different experts. Among the routes of one device's 16 tokens, no expert is named more than 5 times, a bound that some block reaches.
All inputs are finite; a program needn't handle non-finite values.
Results may differ from a plain program's by a relative error of at most 0.0064.
Values may be sent and summed in bfloat16 or wider, within the bound.
No kernel may reach another device: no remote copies, remote signals or barrier semaphores. Data moves between devices by JAX's collectives and lax.ppermute only.
A program may use at most 128 MiB of HBM per device.

v0:
```python
import jax
import jax.numpy as jnp
from jax import lax
from jax.sharding import PartitionSpec as P


def swiglu_back(gate, upper, upstream):
    sigma = jax.nn.sigmoid(gate)
    silu_gate = gate * sigma
    activated = (silu_gate * upper).astype(jnp.bfloat16)
    grad_pre = (upstream * upper * sigma * (1.0 + gate * (1.0 - sigma))).astype(jnp.bfloat16)
    grad_lin = (upstream * silu_gate).astype(jnp.bfloat16)
    return (grad_pre, grad_lin, activated)


def contract_rows(left, right):
    return lax.dot_general(
        left, right, (((0,), (0,)), ((), ())), preferred_element_type=jnp.float32
    )


def exchange(parts, num_dp):
    rows, cols = parts.shape
    parts = parts.reshape(num_dp, rows // num_dp, cols)
    me = lax.axis_index("dp")
    own = lax.dynamic_index_in_dim(parts, me, 0, keepdims=False)
    came = lax.all_to_all(
        parts.astype(jnp.bfloat16), "dp", split_axis=0, concat_axis=0, tiled=True
    )
    others = (jnp.arange(num_dp, dtype=jnp.int32) != me).astype(jnp.float32)
    return own + jnp.sum(came.astype(jnp.float32) * others[:, None, None], axis=0)


def shards(
    activations, cotangent, route_ids, route_weights, gate_weights, up_weights, down_weights
):
    tok_rows, width = activations.shape
    topk = route_ids.shape[1]
    num_dp = lax.axis_size("dp")
    num_exp = lax.axis_size("expert")
    slice_width = gate_weights.shape[1]
    hidden = gate_weights.shape[2]
    capacity = min(tok_rows, 5 * tok_rows * topk // (4 * num_exp))
    flat_ids = route_ids.reshape(-1)
    expert_iota = jnp.arange(num_exp, dtype=jnp.int32)
    onehot = (flat_ids[:, None] == expert_iota[None, :]).astype(jnp.int32)
    before = jnp.cumsum(onehot, axis=0) - onehot
    slot = jnp.sum(before * onehot, axis=1)
    target = (flat_ids * capacity + slot).reshape(tok_rows, topk)
    slot_iota = jnp.arange(num_exp * capacity, dtype=jnp.int32)
    matches = target[:, :, None] == slot_iota[None, None, :]
    placing = jnp.any(matches, axis=1).astype(jnp.bfloat16)
    slot_weight = jnp.sum(jnp.where(matches, route_weights[:, :, None], 0.0), axis=(0, 1))
    by_slice = lambda a: jnp.swapaxes(a.reshape(tok_rows, num_dp, slice_width), 0, 1)
    both = jnp.concatenate([by_slice(activations), by_slice(cotangent)], axis=2)
    slots = placing.T.reshape(num_exp, capacity, tok_rows)
    scale = slot_weight.reshape(num_exp, capacity)
    gate_local = gate_weights[0]
    up_local = up_weights[0]
    down_local = down_weights[0]
    axes = ("dp", "expert")
    split = (capacity + 1) // 2
    bounds = [(0, split), (split, capacity)]
    sums = [None, None, None]
    pieces = []
    for lo, hi in bounds:
        take = hi - lo
        rows = num_exp * take
        pick = jnp.broadcast_to(slots[:, lo:hi].reshape(1, rows, tok_rows), (num_dp, rows, tok_rows))
        gathered_rows = lax.dot_general(
            pick, both, (((2,), (1,)), ((0,), (0,))), preferred_element_type=jnp.float32
        )
        weight = jnp.concatenate(
            [
                jnp.ones((rows, slice_width), jnp.float32),
                jnp.broadcast_to(scale[:, lo:hi].reshape(rows, 1), (rows, slice_width)),
            ],
            axis=1,
        )
        flat_both = (gathered_rows * weight[None]).astype(jnp.bfloat16)
        flat_both = flat_both.reshape(num_dp * num_exp, take, 2 * slice_width)
        recv_both = lax.all_to_all(flat_both, axes, split_axis=0, concat_axis=0, tiled=True)
        recv_both = recv_both.reshape(num_exp * num_dp * take, 2 * slice_width)
        act_rows = recv_both[:, :slice_width]
        cot_rows = recv_both[:, slice_width:]
        gate_part = jnp.dot(act_rows, gate_local, preferred_element_type=jnp.float32)
        up_part = jnp.dot(act_rows, up_local, preferred_element_type=jnp.float32)
        back_part = lax.dot_general(
            cot_rows, down_local, (((1,), (1,)), ((), ())), preferred_element_type=jnp.float32
        )
        summed = exchange(jnp.concatenate([gate_part, up_part, back_part], axis=1), num_dp)
        grad_pre, grad_lin, activated = swiglu_back(
            summed[:, :hidden], summed[:, hidden : 2 * hidden], summed[:, 2 * hidden :]
        )
        gathered = lax.all_gather(
            jnp.concatenate([grad_pre, grad_lin, activated], axis=1), "dp", axis=0, tiled=True
        )
        grad_pre = gathered[:, :hidden]
        grad_lin = gathered[:, hidden : 2 * hidden]
        activated = gathered[:, 2 * hidden :]
        rows_back = lax.dot_general(
            grad_pre, gate_local, (((1,), (1,)), ((), ())), preferred_element_type=jnp.float32
        ) + lax.dot_general(
            grad_lin, up_local, (((1,), (1,)), ((), ())), preferred_element_type=jnp.float32
        )
        terms = (
            contract_rows(act_rows, grad_pre),
            contract_rows(act_rows, grad_lin),
            contract_rows(activated, cot_rows),
        )
        sums = [t if s is None else s + t for s, t in zip(sums, terms)]
        flat_back = rows_back.astype(jnp.bfloat16).reshape(num_dp * num_exp, take, slice_width)
        arrived = lax.all_to_all(flat_back, axes, split_axis=0, concat_axis=0, tiled=True)
        pieces.append(arrived.reshape(num_dp, num_exp, take, slice_width))
    grad_gate, grad_up, grad_down = (s.astype(jnp.bfloat16)[None] for s in sums)
    arrived = jnp.concatenate(pieces, axis=2).reshape(num_dp, num_exp * capacity, slice_width)
    spread = jnp.broadcast_to(placing[None], (num_dp,) + placing.shape)
    grad_slices = lax.dot_general(
        spread, arrived, (((2,), (1,)), ((0,), (0,))), preferred_element_type=jnp.float32
    ).astype(jnp.bfloat16)
    grad_input = jnp.swapaxes(grad_slices, 0, 1).reshape(tok_rows, width)
    return (grad_input, grad_gate, grad_up, grad_down)


def solution(mesh):
    placed = (
        P(("expert", "dp"), None),
        P(("expert", "dp"), None),
        P(("expert", "dp"), None),
        P(("expert", "dp"), None),
        P("expert", "dp", None),
        P("expert", "dp", None),
        P("expert", None, "dp"),
    )
    return jax.shard_map(
        shards,
        mesh=mesh,
        in_specs=placed,
        out_specs=(
            P(("expert", "dp"), None),
            P("expert", "dp", None),
            P("expert", "dp", None),
            P("expert", None, "dp"),
        ),
        check_vma=False,
    )
```

profile of v0, /device:TPU:1, one launch (start us, length us, event | category | flops | bytes accessed | tf_op | source)
XLA Modules:
  0.0 282.3 jit_solution(14984752875423337022)
XLA Ops:
  10.3 1.1 bitcast_bitcast_fusion
  12.1 1.6 reshape.96
  13.7 11.9 %all-to-all-start.3 = ((bf16[128,2,3584]{2,1,0:T(2,128)(2,1)}), bf16[128,2,3584]{2,1,0:T(2,128)(2,1)}, u32[]{:S(2)}, u32[]{:S(2)}) async-start(bf16[128,2,3584]{2,1,0:T(2,128)(2,1)} %reshape.96), calls=%async_computation.3 | async-start | bytes 3670016 | tf_op jit(solution)/shard_map/all_to_all | solution.py:82
  26.1 0.9 fusion
  27.0 4.0 %reshape.91 = bf16[128,3,3584]{2,1,0:T(4,128)(2,1)} reshape(bf16[4,96,3584]{2,1,0:T(8,128)(2,1)S(1)} %fusion) | data formatting | bytes 5505024 | tf_op jit(solution)/shard_map/reshape | solution.py:81
  31.1 21.9 %all-to-all-done.3 = bf16[128,2,3584]{2,1,0:T(2,128)(2,1)} async-done(((bf16[128,2,3584]{2,1,0:T(2,128)(2,1)}), bf16[128,2,3584]{2,1,0:T(2,128)(2,1)}, u32[]{:S(2)}, u32[]{:S(2)}) %all-to-all-start.3) | async-done | bytes 1835040 | tf_op jit(solution)/shard_map/all_to_all | solution.py:82
  53.0 5.7 %all-to-all-start = ((bf16[128,3,3584]{2,1,0:T(4,128)(2,1)}), bf16[128,3,3584]{2,1,0:T(4,128)(2,1)}, u32[]{:S(2)}, u32[]{:S(2)}) async-start(bf16[128,3,3584]{2,1,0:T(4,128)(2,1)} %reshape.91), calls=%async_computation | async-start | bytes 7340032 | tf_op jit(solution)/shard_map/all_to_all | solution.py:82
  58.7 4.1 %reshape.97 = bf16[256,3584]{1,0:T(8,128)(2,1)S(1)} reshape(bf16[128,2,3584]{2,1,0:T(2,128)(2,1)} %all-to-all-done.3) | data formatting | bytes 3670016 | tf_op jit(solution)/shard_map/reshape | solution.py:83
  62.8 3.8 %fusion.8 = f32[256,1024]{1,0:T(8,128)S(1)} fusion(bf16[1,1792,1024]{2,1,0:T(8,128)(2,1)} %param.12, bf16[256,3584]{1,0:T(8,128)(2,1)S(1)} %reshape.97), kind=kOutput, calls=%fused_computation.15 | convolution fusion | flops 939524096 | bytes 5636096 | tf_op jit(solution)/shard_map/dot_general | solution.py:87
  66.7 1.1 fusion.2
  67.8 0.9 copy-done.9
  68.7 1.2 fusion.16
  70.2 1.7 copy-done.1
  71.9 1.4 convert_element_type.92
  73.3 32.6 %all-to-all-done = bf16[128,3,3584]{2,1,0:T(4,128)(2,1)} async-done(((bf16[128,3,3584]{2,1,0:T(4,128)(2,1)}), bf16[128,3,3584]{2,1,0:T(4,128)(2,1)}, u32[]{:S(2)}, u32[]{:S(2)}) %all-to-all-start) | async-done | bytes 2752544 | tf_op jit(solution)/shard_map/all_to_all | solution.py:82
  105.9 4.5 %all-to-all-start.4 = ((bf16[4,64,3072]{2,1,0:T(8,128)(2,1)}), bf16[4,64,3072]{2,1,0:T(8,128)(2,1)}, u32[]{:S(2)}, u32[]{:S(2)}) async-start(bf16[4,64,3072]{2,1,0:T(8,128)(2,1)} %convert_element_type.92), calls=%async_computation.4 | async-start | bytes 3145728 | tf_op jit(solution)/shard_map/all_to_all | solution.py:27
  110.4 5.6 %reshape.92 = bf16[384,3584]{1,0:T(8,128)(2,1)S(1)} reshape(bf16[128,3,3584]{2,1,0:T(4,128)(2,1)} %all-to-all-done) | data formatting | bytes 5505024 | tf_op jit(solution)/shard_map/reshape | solution.py:83
  116.1 3.8 %fusion.12 = f32[384,1024]{1,0:T(8,128)S(1)} fusion(bf16[1,1792,1024]{2,1,0:T(8,128)(2,1)} %param.12, bf16[384,3584]{1,0:T(8,128)(2,1)S(1)} %reshape.92), kind=kOutput, calls=%fused_computation.19 | convolution fusion | flops 1409286144 | bytes 6619136 | tf_op jit(solution)/shard_map/dot_general | solution.py:87
  119.9 1.6 fusion.4
  121.9 1.7 fusion.20
  124.1 2.1 copy-done
  126.3 1.7 convert_element_type.84
  128.0 2.0 all-to-all-done.4
  130.0 4.5 %all-to-all-start.1 = ((bf16[4,96,3072]{2,1,0:T(8,128)(2,1)}), bf16[4,96,3072]{2,1,0:T(8,128)(2,1)}, u32[]{:S(2)}, u32[]{:S(2)}) async-start(bf16[4,96,3072]{2,1,0:T(8,128)(2,1)} %convert_element_type.84), calls=%async_computation.1 | async-start | bytes 4718592 | tf_op jit(solution)/shard_map/all_to_all | solution.py:27
  134.6 1.9 multiply_reduce_fusion.1
  136.5 1.3 bitcast_add_fusion.1
  138.7 33.0 %all-to-all-done.1 = bf16[4,96,3072]{2,1,0:T(8,128)(2,1)} async-done(((bf16[4,96,3072]{2,1,0:T(8,128)(2,1)}), bf16[4,96,3072]{2,1,0:T(8,128)(2,1)}, u32[]{:S(2)}, u32[]{:S(2)}) %all-to-all-start.1) | async-done | bytes 2359328 | tf_op jit(solution)/shard_map/all_to_all | solution.py:27
  171.8 2.4 multiply_reduce_fusion
  174.1 1.4 bitcast_add_fusion
  175.8 0.9 pad_maximum_fusion.3
  176.7 3.5 %fusion.6 = f32[256,1792]{1,0:T(8,128)S(1)} fusion(bf16[1,1792,1024]{2,1,0:T(8,128)(2,1)} %param.12, bf16[256,3072]{1,0:T(8,128)(2,1)} %all-gather.5.cloned.1.call-done), kind=kOutput, calls=%fused_computation.13 | convolution fusion | flops 939524096 | bytes 6029312 | tf_op jit(solution)/shard_map/dot_general | solution.py:103
  180.3 3.1 %fusion.34 = bf16[256,1792]{1,0:T(8,128)(2,1)} fusion(f32[256,1792]{1,0:T(8,128)S(1)} %fusion.6, bf16[1,1792,1024]{2,1,0:T(8,128)(2,1)S(1)} %copy-done.11, bf16[256,3072]{1,0:T(8,128)(2,1)} %all-gather.5.cloned.1.call-done), kind=kOutput, calls=%fused_computation.37 | convolution fusion | flops 940441600 | bytes 6946816 | tf_op jit(solution)/shard_map/dot_general | solution.py:101
  183.4 3.1 %reshape.99 = bf16[128,2,1792]{2,1,0:T(2,128)(2,1)} reshape(bf16[256,1792]{1,0:T(8,128)(2,1)} %fusion.34) | data formatting | bytes 1835008 | tf_op jit(solution)/shard_map/reshape | solution.py:112
  186.5 37.3 %all_to_all.30 = bf16[128,2,1792]{2,1,0:T(2,128)(2,1)S(1)} all-to-all(bf16[128,2,1792]{2,1,0:T(2,128)(2,1)} %reshape.99), channel_id=1, replica_groups=mesh['expert'=32,'dp'=4] {'dp','expert'}, dimensions={0} | all-to-all | bytes 1835008 | tf_op jit(solution)/shard_map/all_to_all | solution.py:113
  223.7 1.6 copy.61
  225.4 4.1 %fusion.10 = f32[384,1792]{1,0:T(8,128)S(1)} fusion(bf16[1,1792,1024]{2,1,0:T(8,128)(2,1)} %param.12, bf16[384,3072]{1,0:T(8,128)(2,1)} %all-gather.3.cloned.1.call-done), kind=kOutput, calls=%fused_computation.17 | convolution fusion | flops 1409286144 | bytes 7208960 | tf_op jit(solution)/shard_map/dot_general | solution.py:103
  229.4 3.9 %fusion.28 = bf16[384,1792]{1,0:T(8,128)(2,1)} fusion(f32[384,1792]{1,0:T(8,128)S(1)} %fusion.10, bf16[1,1792,1024]{2,1,0:T(8,128)(2,1)S(1)} %copy-done.12, bf16[384,3072]{1,0:T(8,128)(2,1)} %all-gather.3.cloned.1.call-done), kind=kOutput, calls=%fused_computation.35 | convolution fusion | flops 1410662400 | bytes 8585216 | tf_op jit(solution)/shard_map/dot_general | solution.py:101
  233.3 3.9 %reshape.94 = bf16[128,3,1792]{2,1,0:T(4,128)(2,1)} reshape(bf16[384,1792]{1,0:T(8,128)(2,1)} %fusion.28) | data formatting | bytes 2752512 | tf_op jit(solution)/shard_map/reshape | solution.py:112
  237.2 5.6 %all-to-all-start.2 = ((bf16[128,3,1792]{2,1,0:T(4,128)(2,1)}), bf16[128,3,1792]{2,1,0:T(4,128)(2,1)}, u32[]{:S(2)}, u32[]{:S(2)}) async-start(bf16[128,3,1792]{2,1,0:T(4,128)(2,1)} %reshape.94), calls=%async_computation.2 | async-start | bytes 3670016 | tf_op jit(solution)/shard_map/all_to_all | solution.py:113
  242.8 3.4 %fusion.46 = f32[1792,1024]{1,0:T(8,128)S(1)} fusion(bf16[384,3584]{1,0:T(8,128)(2,1)S(1)} %reshape.92, bf16[384,3072]{1,0:T(8,128)(2,1)} %all-gather.3.cloned.1.call-done), kind=kOutput, calls=%fused_computation.48 | convolution fusion | flops 1409286144 | bytes 9502720 | tf_op jit(solution)/shard_map/dot_general | solution.py:17
  246.2 2.1 fusion.44
  248.4 3.0 %fusion.22 = bf16[1,1792,1024]{2,1,0:T(8,128)(2,1)} fusion(f32[1792,1024]{1,0:T(8,128)S(1)} %fusion.46, bf16[256,3584]{1,0:T(8,128)(2,1)S(1)} %copy-done.3, bf16[256,3072]{1,0:T(8,128)(2,1)S(1)} %copy-done.6), kind=kOutput, calls=%fused_computation.29 | convolution fusion | flops 943194112 | bytes 12451840 | tf_op jit(solution)/shard_map/dot_general | solution.py:17
  251.4 2.1 fusion.41
  253.5 3.0 %fusion.23 = bf16[1,1792,1024]{2,1,0:T(8,128)(2,1)} fusion(f32[1792,1024]{1,0:T(8,128)S(1)} %fusion.44, bf16[256,3584]{1,0:T(8,128)(2,1)S(1)} %copy-done.3, bf16[256,3072]{1,0:T(8,128)(2,1)S(1)} %copy-done.6), kind=kOutput, calls=%fused_computation.30 | convolution fusion | flops 943194112 | bytes 12451840 | tf_op jit(solution)/shard_map/dot_general | solution.py:17
  256.5 3.0 %fusion.24 = bf16[1,1024,1792]{2,1,0:T(8,128)(2,1)} fusion(f32[1024,1792]{1,0:T(8,128)S(1)} %fusion.41, bf16[256,3584]{1,0:T(8,128)(2,1)S(1)} %copy-done.3, bf16[256,3072]{1,0:T(8,128)(2,1)S(1)} %copy-done.6), kind=kOutput, calls=%fused_computation.31 | convolution fusion | flops 943194112 | bytes 12451840 | tf_op jit(solution)/shard_map/dot_general | solution.py:17
  259.5 10.5 %all-to-all-done.2 = bf16[128,3,1792]{2,1,0:T(4,128)(2,1)} async-done(((bf16[128,3,1792]{2,1,0:T(4,128)(2,1)}), bf16[128,3,1792]{2,1,0:T(4,128)(2,1)}, u32[]{:S(2)}, u32[]{:S(2)}) %all-to-all-start.2) | async-done | bytes 1376288 | tf_op jit(solution)/shard_map/all_to_all | solution.py:113
  270.0 2.8 copy.60
  272.8 1.5 pad_maximum_fusion.2
  (64 shorter events, 7.9 us)
Async XLA Ops:
  13.7 39.2 %all-to-all-start.3 = ((bf16[128,2,3584]{2,1,0:T(2,128)(2,1)}), bf16[128,2,3584]{2,1,0:T(2,128)(2,1)}, u32[]{:S(2)}, u32[]{:S(2)}) async-start(bf16[128,2,3584]{2,1,0:T(2,128)(2,1)} %reshape.96), calls=%async_computation.3 | async-start | bytes 3670016 | tf_op jit(solution)/shard_map/all_to_all | solution.py:82
  53.0 53.0 %all-to-all-start = ((bf16[128,3,3584]{2,1,0:T(4,128)(2,1)}), bf16[128,3,3584]{2,1,0:T(4,128)(2,1)}, u32[]{:S(2)}, u32[]{:S(2)}) async-start(bf16[128,3,3584]{2,1,0:T(4,128)(2,1)} %reshape.91), calls=%async_computation | async-start | bytes 7340032 | tf_op jit(solution)/shard_map/all_to_all | solution.py:82
  62.7 5.0 %copy-start.2 = (bf16[256,3584]{1,0:T(8,128)(2,1)}, bf16[256,3584]{1,0:T(8,128)(2,1)S(1)}, u32[]{:S(2)}) copy-start(bf16[256,3584]{1,0:T(8,128)(2,1)S(1)} %reshape.97) | copy-start | bytes 5505028
  62.8 3.9 %copy-start.7 = (bf16[1,1024,1792]{2,1,0:T(8,128)(2,1)S(1)}, bf16[1,1024,1792]{2,1,0:T(8,128)(2,1)}, u32[]{:S(2)}) copy-start(bf16[1,1024,1792]{2,1,0:T(8,128)(2,1)} %param.13) | copy-start | bytes 11010052
  66.6 2.0 copy-start.9
  70.2 1.7 copy-start.1
  105.9 24.1 %all-to-all-start.4 = ((bf16[4,64,3072]{2,1,0:T(8,128)(2,1)}), bf16[4,64,3072]{2,1,0:T(8,128)(2,1)}, u32[]{:S(2)}, u32[]{:S(2)}) async-start(bf16[4,64,3072]{2,1,0:T(8,128)(2,1)} %convert_element_type.92), calls=%async_computation.4 | async-start | bytes 3145728 | tf_op jit(solution)/shard_map/all_to_all | solution.py:27
  116.1 3.8 %copy-start.8 = (bf16[1,1024,1792]{2,1,0:T(8,128)(2,1)S(1)}, bf16[1,1024,1792]{2,1,0:T(8,128)(2,1)}, u32[]{:S(2)}) copy-start(bf16[1,1024,1792]{2,1,0:T(8,128)(2,1)} %param.13) | copy-start | bytes 11010052
  119.9 2.0 copy-start.10
  124.1 2.1 copy-start
  130.0 41.7 %all-to-all-start.1 = ((bf16[4,96,3072]{2,1,0:T(8,128)(2,1)}), bf16[4,96,3072]{2,1,0:T(8,128)(2,1)}, u32[]{:S(2)}, u32[]{:S(2)}) async-start(bf16[4,96,3072]{2,1,0:T(8,128)(2,1)} %convert_element_type.84), calls=%async_computation.1 | async-start | bytes 4718592 | tf_op jit(solution)/shard_map/all_to_all | solution.py:27
  134.5 42.2 %all-gather.5.cloned.1.call-start = ((), (), s32[]{:S(2)}) async-start(), calls=%async_computation.7 | async-start | bytes 1966080 | tf_op jit(solution)/shard_map/all_gather | solution.py:95
  138.7 86.7 %all-gather.3.cloned.1.call-start = ((), (), s32[]{:S(2)}) async-start(), calls=%async_computation.6 | async-start | bytes 2949120 | tf_op jit(solution)/shard_map/all_gather | solution.py:95
  176.7 3.5 %copy-start.11 = (bf16[1,1792,1024]{2,1,0:T(8,128)(2,1)S(1)}, bf16[1,1792,1024]{2,1,0:T(8,128)(2,1)}, u32[]{:S(2)}) copy-start(bf16[1,1792,1024]{2,1,0:T(8,128)(2,1)} %param.11) | copy-start | bytes 11010052
  225.4 4.1 %copy-start.12 = (bf16[1,1792,1024]{2,1,0:T(8,128)(2,1)S(1)}, bf16[1,1792,1024]{2,1,0:T(8,128)(2,1)}, u32[]{:S(2)}) copy-start(bf16[1,1792,1024]{2,1,0:T(8,128)(2,1)} %param.11) | copy-start | bytes 11010052
  237.2 32.9 %all-to-all-start.2 = ((bf16[128,3,1792]{2,1,0:T(4,128)(2,1)}), bf16[128,3,1792]{2,1,0:T(4,128)(2,1)}, u32[]{:S(2)}, u32[]{:S(2)}) async-start(bf16[128,3,1792]{2,1,0:T(4,128)(2,1)} %reshape.94), calls=%async_computation.2 | async-start | bytes 3670016 | tf_op jit(solution)/shard_map/all_to_all | solution.py:113
  242.8 3.4 %copy-start.5 = (bf16[384,3072]{1,0:T(8,128)(2,1)S(1)}, bf16[384,3072]{1,0:T(8,128)(2,1)}, u32[]{:S(2)}) copy-start(bf16[384,3072]{1,0:T(8,128)(2,1)} %all-gather.3.cloned.1.call-done) | copy-start | bytes 7077892
  246.2 2.1 copy-start.3
  246.2 2.1 copy-start.6
  259.5 13.3 %copy-start.4 = (bf16[4,32,2,1792]{3,0,2,1:T(4,128)(2,1)S(1)}, bf16[4,32,2,1792]{3,0,2,1:T(4,128)(2,1)}, u32[]{:S(2)}) copy-start(bf16[4,32,2,1792]{3,0,2,1:T(4,128)(2,1)} %copy.61) | copy-start | bytes 2752516
Sparse Core Ops, SparseCore 0:
  138.8 36.6 all-gather.4
  177.2 41.7 all-gather.2
where the time goes:
time: 283 us; the launch traced here: 282 us
  waiting for transfers between devices  100 us (35%)
  matrix products  46.5 us (16%)
  blocking collectives  37.3 us (13%)
  local copies, waits for them, and re-layouts  36.5 us (13%)
  starting transfers between devices  32.3 us (11%)
  other arithmetic  15.1 us (5%)
  between operations  14.5 us (5%)
    all_to_all x2, waiting for transfers between devices, shards(): lax.all_to_all(flat_both, axes, split_axis=0, concat_axis=0, tiled=True)  54.5 us
    all_to_all x1, blocking collectives, shards(): lax.all_to_all(flat_back, axes, split_axis=0, concat_axis=0, tiled=True)  37.3 us
    all_to_all x2, waiting for transfers between devices, exchange(): lax.all_to_all(parts.astype(jnp.bfloat16), 'dp', split_axis=0, concat_axi...  35.1 us
    all_to_all x2, starting transfers between devices, shards(): lax.all_to_all(flat_both, axes, split_axis=0, concat_axis=0, tiled=True)  17.6 us
    dot_general x6, matrix products, contract_rows(): lax.dot_general(left, right, (((0,), (0,)), ((), ())), preferred_element_...  16.6 us
    all_to_all x1, waiting for transfers between devices, shards(): lax.all_to_all(flat_back, axes, split_axis=0, concat_axis=0, tiled=True)  10.5 us
    reshape x2, local copies, waits for them, and re-layouts, shards(): recv_both = recv_both.reshape(num_exp * num_dp * take, 2 * slice_width)  9.71 us
    all_to_all x2, starting transfers between devices, exchange(): lax.all_to_all(parts.astype(jnp.bfloat16), 'dp', split_axis=0, concat_axi...  9.02 us
  transfers between devices with their start and end apart: 7, of which 5 were waited for; matrix products, arithmetic and copies ran while one was open for 25% of the time, Pallas kernels for 0%

commit v1 on v0

--- a/solution.py
+++ b/solution.py
@@ -20,15 +20,7 @@
 
 
 def exchange(parts, num_dp):
-    rows, cols = parts.shape
-    parts = parts.reshape(num_dp, rows // num_dp, cols)
-    me = lax.axis_index("dp")
-    own = lax.dynamic_index_in_dim(parts, me, 0, keepdims=False)
-    came = lax.all_to_all(
-        parts.astype(jnp.bfloat16), "dp", split_axis=0, concat_axis=0, tiled=True
-    )
-    others = (jnp.arange(num_dp, dtype=jnp.int32) != me).astype(jnp.float32)
-    return own + jnp.sum(came.astype(jnp.float32) * others[:, None, None], axis=0)
+    return lax.psum_scatter(parts, "dp", scatter_dimension=0, tiled=True)
 
 
 def shards(

time: 283 us -> 340 us (1.20)
  blocking collectives: 37.3 us -> 148 us
  starting transfers between devices: 32.3 us -> 6.14 us
  waiting for transfers between devices: 100 us -> 80.4 us
  other arithmetic: 15.1 us -> 11 us
  local copies, waits for them, and re-layouts: 36.5 us -> 32.8 us
    all_to_all x0 -> x2, blocking collectives: none -> 112 us  [shards(): lax.all_to_all(flat_both, axes, split_axis=0, concat_axis=0, tiled=True)]
    all_to_all x4 -> x0, waiting for transfers between devices: 89.6 us -> none  [the longest x2 54.5 us: shards(): lax.all_to_all(flat_both, axes, split_axis=0, concat_axis=0, tiled=True)]
    reduce_scatter x0 -> x2, waiting for transfers between devices: none -> 43.9 us  [exchange(): return lax.psum_scatter(parts, 'dp', scatter_dimension=0, tiled=True)]
    all_to_all x4 -> x0, starting transfers between devices: 26.6 us -> none  [the longest x2 17.6 us: shards(): lax.all_to_all(flat_both, axes, split_axis=0, concat_axis=0, tiled=True)]
    all_gather x2, waiting for transfers between devices: 0.02 us -> 26 us  [shards(): lax.all_gather(jnp.concatenate([grad_pre, grad_lin, activated], axis=1),...]
    reduce_sum x2 -> x0, other arithmetic: 4.27 us -> none  [exchange(): jnp.sum(came.astype(jnp.float32) * others[:, None, None], axis=0)]
    unnamed x28 -> x24, local copies, waits for them, and re-layouts: 6.65 us -> 2.86 us
    concatenate x2, other arithmetic: 0.85 us -> 4.46 us  [shards(): jnp.concatenate([gate_part, up_part, back_part], axis=1)]
  transfers between devices with their start and end apart: 7 -> 5, of which waited for: 5 -> 3; matrix products, arithmetic and copies ran while one was open for 25% -> 16% of each run, Pallas kernels for 0% -> 0%
where the time goes in v1:
time: 340 us; the launch traced here: 339 us
  blocking collectives  148 us (44%)
  waiting for transfers between devices  80.4 us (24%)
  matrix products  46.3 us (14%)
  local copies, waits for them, and re-layouts  32.8 us (10%)
  between operations  14.2 us (4%)
  other arithmetic  11 us (3%)
  starting transfers between devices  6.14 us (2%)
    all_to_all x2, blocking collectives, shards(): lax.all_to_all(flat_both, axes, split_axis=0, concat_axis=0, tiled=True)  112 us
    reduce_scatter x2, waiting for transfers between devices, exchange(): return lax.psum_scatter(parts, 'dp', scatter_dimension=0, tiled=True)  43.9 us
    all_to_all x1, blocking collectives, shards(): lax.all_to_all(flat_back, axes, split_axis=0, concat_axis=0, tiled=True)  36.6 us
    all_gather x2, waiting for transfers between devices, shards(): lax.all_gather(jnp.concatenate([grad_pre, grad_lin, activated], axis=1),...  26 us
    dot_general x6, matrix products, contract_rows(): lax.dot_general(left, right, (((0,), (0,)), ((), ())), preferred_element_...  16.6 us
    all_to_all x1, waiting for transfers between devices, shards(): lax.all_to_all(flat_back, axes, split_axis=0, concat_axis=0, tiled=True)  10.5 us
    reshape x2, local copies, waits for them, and re-layouts, shards(): recv_both = recv_both.reshape(num_exp * num_dp * take, 2 * slice_width)  9.7 us
    dot_general x2, matrix products, shards(): up_part = jnp.dot(act_rows, up_local, preferred_element_type=jnp.float32)  7.62 us
  transfers between devices with their start and end apart: 5, of which 3 were waited for; matrix products, arithmetic and copies ran while one was open for 16% of the time, Pallas kernels for 0%

profile of v1, /device:TPU:1, one launch (start us, length us, event | category | flops | bytes accessed | tf_op | source)
XLA Modules:
  0.0 339.0 jit_solution(4906502265938485249)
XLA Ops:
  7.2 0.8 copy.51
  8.1 0.8 copy.57
  10.4 1.1 bitcast_bitcast_fusion
  11.4 0.7 fusion.1
  12.1 1.6 reshape.84
  13.8 39.2 %all_to_all.20 = bf16[128,2,3584]{2,1,0:T(2,128)(2,1)} all-to-all(bf16[128,2,3584]{2,1,0:T(2,128)(2,1)} %reshape.84), channel_id=1, replica_groups=mesh['expert'=32,'dp'=4] {'dp','expert'}, dimensions={0} | all-to-all | bytes 3670016 | tf_op jit(solution)/shard_map/all_to_all | solution.py:74
  53.0 4.1 %reshape.85 = bf16[256,3584]{1,0:T(8,128)(2,1)S(1)} reshape(bf16[128,2,3584]{2,1,0:T(2,128)(2,1)} %all_to_all.20) | data formatting | bytes 3670016 | tf_op jit(solution)/shard_map/reshape | solution.py:75
  57.1 3.8 %fusion.8 = f32[256,1024]{1,0:T(8,128)S(1)} fusion(bf16[1,1792,1024]{2,1,0:T(8,128)(2,1)} %param.12, bf16[256,3584]{1,0:T(8,128)(2,1)S(1)} %reshape.85), kind=kOutput, calls=%fused_computation.14 | convolution fusion | flops 939524096 | bytes 5636096 | tf_op jit(solution)/shard_map/dot_general | solution.py:79
  61.0 1.1 fusion.2
  62.1 0.9 copy-done.7
  63.0 1.1 fusion.16
  64.1 2.0 pad_maximum_fusion.1
  66.7 0.9 fusion
  67.6 4.0 %reshape.80 = bf16[128,3,3584]{2,1,0:T(4,128)(2,1)} reshape(bf16[4,96,3584]{2,1,0:T(8,128)(2,1)S(1)} %fusion) | data formatting | bytes 5505024 | tf_op jit(solution)/shard_map/reshape | solution.py:73
  71.6 72.4 %all_to_all.21 = bf16[128,3,3584]{2,1,0:T(4,128)(2,1)} all-to-all(bf16[128,3,3584]{2,1,0:T(4,128)(2,1)} %reshape.80), channel_id=1, replica_groups=mesh['expert'=32,'dp'=4] {'dp','expert'}, dimensions={0} | all-to-all | bytes 5505024 | tf_op jit(solution)/shard_map/all_to_all | solution.py:74
  144.0 5.6 %reshape.81 = bf16[384,3584]{1,0:T(8,128)(2,1)S(1)} reshape(bf16[128,3,3584]{2,1,0:T(4,128)(2,1)} %all_to_all.21) | data formatting | bytes 5505024 | tf_op jit(solution)/shard_map/reshape | solution.py:75
  149.7 3.8 %fusion.12 = f32[384,1024]{1,0:T(8,128)S(1)} fusion(bf16[1,1792,1024]{2,1,0:T(8,128)(2,1)} %param.12, bf16[384,3584]{1,0:T(8,128)(2,1)S(1)} %reshape.81), kind=kOutput, calls=%fused_computation.18 | convolution fusion | flops 1409286144 | bytes 6619136 | tf_op jit(solution)/shard_map/dot_general | solution.py:79
  153.5 1.6 fusion.4
  155.1 0.4 copy-done.8
  155.5 1.7 fusion.20
  157.2 2.4 pad_maximum_fusion
  159.7 0.2 all-gather.5.cloned.1.call-start
  159.9 1.3 multiply_convert_fusion.5
  161.2 0.8 pad_maximum_fusion.5
  162.0 43.8 %reduce-scatter.3.cloned.1.call-done = f32[96,3072]{1,0:T(8,128)} async-done(((f32[384,3072]{1,0:T(8,128)}), f32[96,3072]{1,0:T(8,128)}) %reduce-scatter.3.cloned.1.call-update) | async-done | bytes 1179664 | tf_op jit(solution)/shard_map/reduce_scatter | solution.py:23
  205.9 1.5 multiply_convert_fusion.2
  207.3 0.9 pad_maximum_fusion.3
  208.2 26.0 %all-gather.5.cloned.1.call-done = bf16[256,3072]{1,0:T(8,128)(2,1)} async-done(((bf16[64,3072]{1,0:T(8,128)(2,1)}), bf16[256,3072]{1,0:T(8,128)(2,1)}) %all-gather.5.cloned.1.call-update) | async-done | bytes 1572880 | tf_op jit(solution)/shard_map/all_gather | solution.py:87
  234.2 3.5 %fusion.6 = f32[256,1792]{1,0:T(8,128)S(1)} fusion(bf16[1,1792,1024]{2,1,0:T(8,128)(2,1)} %param.12, bf16[256,3072]{1,0:T(8,128)(2,1)} %all-gather.5.cloned.1.call-done), kind=kOutput, calls=%fused_computation.12 | convolution fusion | flops 939524096 | bytes 6029312 | tf_op jit(solution)/shard_map/dot_general | solution.py:95
  237.7 3.1 fusion.34
  240.9 3.1 reshape.86
  243.9 36.6 %all_to_all.22 = bf16[128,2,1792]{2,1,0:T(2,128)(2,1)S(1)} all-to-all(bf16[128,2,1792]{2,1,0:T(2,128)(2,1)} %reshape.86), channel_id=1, replica_groups=mesh['expert'=32,'dp'=4] {'dp','expert'}, dimensions={0} | all-to-all | bytes 1835008 | tf_op jit(solution)/shard_map/all_to_all | solution.py:105
  280.5 1.7 copy.61
  282.2 4.0 %fusion.10 = f32[384,1792]{1,0:T(8,128)S(1)} fusion(bf16[1,1792,1024]{2,1,0:T(8,128)(2,1)} %param.12, bf16[384,3072]{1,0:T(8,128)(2,1)} %all-gather.3.cloned.1.call-done), kind=kOutput, calls=%fused_computation.16 | convolution fusion | flops 1409286144 | bytes 7208960 | tf_op jit(solution)/shard_map/dot_general | solution.py:95
  286.3 3.9 %fusion.28 = bf16[384,1792]{1,0:T(8,128)(2,1)} fusion(f32[384,1792]{1,0:T(8,128)S(1)} %fusion.10, bf16[1,1792,1024]{2,1,0:T(8,128)(2,1)S(1)} %copy-done.10, bf16[384,3072]{1,0:T(8,128)(2,1)} %all-gather.3.cloned.1.call-done), kind=kOutput, calls=%fused_computation.33 | convolution fusion | flops 1410662400 | bytes 8585216 | tf_op jit(solution)/shard_map/dot_general | solution.py:93
  290.2 3.9 %reshape.82 = bf16[128,3,1792]{2,1,0:T(4,128)(2,1)} reshape(bf16[384,1792]{1,0:T(8,128)(2,1)} %fusion.28) | data formatting | bytes 2752512 | tf_op jit(solution)/shard_map/reshape | solution.py:104
  294.0 5.8 %all-to-all-start.1 = ((bf16[128,3,1792]{2,1,0:T(4,128)(2,1)}), bf16[128,3,1792]{2,1,0:T(4,128)(2,1)}, u32[]{:S(2)}, u32[]{:S(2)}) async-start(bf16[128,3,1792]{2,1,0:T(4,128)(2,1)} %reshape.82), calls=%async_computation.2 | async-start | bytes 3670016 | tf_op jit(solution)/shard_map/all_to_all | solution.py:105
  299.8 3.4 fusion.46
  303.3 2.1 fusion.44
  305.4 3.0 fusion.22
  308.4 2.1 fusion.41
  310.5 3.0 fusion.23
  313.5 3.0 fusion.24
  316.5 10.5 %all-to-all-done.1 = bf16[128,3,1792]{2,1,0:T(4,128)(2,1)} async-done(((bf16[128,3,1792]{2,1,0:T(4,128)(2,1)}), bf16[128,3,1792]{2,1,0:T(4,128)(2,1)}, u32[]{:S(2)}, u32[]{:S(2)}) %all-to-all-start.1) | async-done | bytes 1376288 | tf_op jit(solution)/shard_map/all_to_all | solution.py:105
  327.1 2.8 copy.60
  329.9 1.5 pad_maximum_fusion.2
  331.4 0.4 fusion.38
  331.8 0.7 copy.68
  (53 shorter events, 2.3 us)
Async XLA Ops:
  7.2 152.7 %reduce-scatter.5.cloned.1.call-start = ((), (), s32[]{:S(2)}) async-start(), calls=%async_computation.8 | async-start | bytes 3932160 | tf_op jit(solution)/shard_map/reduce_scatter | solution.py:23
  57.1 5.0 %copy-start = (bf16[256,3584]{1,0:T(8,128)(2,1)}, bf16[256,3584]{1,0:T(8,128)(2,1)S(1)}, u32[]{:S(2)}) copy-start(bf16[256,3584]{1,0:T(8,128)(2,1)S(1)} %reshape.85) | copy-start | bytes 5505028
  57.1 3.9 %copy-start.5 = (bf16[1,1024,1792]{2,1,0:T(8,128)(2,1)S(1)}, bf16[1,1024,1792]{2,1,0:T(8,128)(2,1)}, u32[]{:S(2)}) copy-start(bf16[1,1024,1792]{2,1,0:T(8,128)(2,1)} %param.13) | copy-start | bytes 11010052
  60.9 2.0 copy-start.7
  66.1 139.7 %reduce-scatter.3.cloned.1.call-start = ((), (), s32[]{:S(2)}) async-start(), calls=%async_computation.6 | async-start | bytes 5898240 | tf_op jit(solution)/shard_map/reduce_scatter | solution.py:23
  149.7 3.8 %copy-start.6 = (bf16[1,1024,1792]{2,1,0:T(8,128)(2,1)S(1)}, bf16[1,1024,1792]{2,1,0:T(8,128)(2,1)}, u32[]{:S(2)}) copy-start(bf16[1,1024,1792]{2,1,0:T(8,128)(2,1)} %param.13) | copy-start | bytes 11010052
  153.5 2.0 copy-start.8
  159.7 74.6 %all-gather.5.cloned.1.call-start = ((), (), s32[]{:S(2)}) async-start(), calls=%async_computation.9 | async-start | bytes 1966080 | tf_op jit(solution)/shard_map/all_gather | solution.py:87
  162.0 120.2 %all-gather.3.cloned.1.call-start = ((), (), s32[]{:S(2)}) async-start(), calls=%async_computation.7 | async-start | bytes 2949120 | tf_op jit(solution)/shard_map/all_gather | solution.py:87
  234.2 3.5 %copy-start.9 = (bf16[1,1792,1024]{2,1,0:T(8,128)(2,1)S(1)}, bf16[1,1792,1024]{2,1,0:T(8,128)(2,1)}, u32[]{:S(2)}) copy-start(bf16[1,1792,1024]{2,1,0:T(8,128)(2,1)} %param.11) | copy-start | bytes 11010052
  282.2 4.1 %copy-start.10 = (bf16[1,1792,1024]{2,1,0:T(8,128)(2,1)S(1)}, bf16[1,1792,1024]{2,1,0:T(8,128)(2,1)}, u32[]{:S(2)}) copy-start(bf16[1,1792,1024]{2,1,0:T(8,128)(2,1)} %param.11) | copy-start | bytes 11010052
  294.0 33.0 %all-to-all-start.1 = ((bf16[128,3,1792]{2,1,0:T(4,128)(2,1)}), bf16[128,3,1792]{2,1,0:T(4,128)(2,1)}, u32[]{:S(2)}, u32[]{:S(2)}) async-start(bf16[128,3,1792]{2,1,0:T(4,128)(2,1)} %reshape.82), calls=%async_computation.2 | async-start | bytes 3670016 | tf_op jit(solution)/shard_map/all_to_all | solution.py:105
  299.8 3.4 %copy-start.3 = (bf16[384,3072]{1,0:T(8,128)(2,1)S(1)}, bf16[384,3072]{1,0:T(8,128)(2,1)}, u32[]{:S(2)}) copy-start(bf16[384,3072]{1,0:T(8,128)(2,1)} %all-gather.3.cloned.1.call-done) | copy-start | bytes 7077892
  303.2 2.1 copy-start.1
  303.2 2.1 copy-start.4
  316.5 13.3 %copy-start.2 = (bf16[4,32,2,1792]{3,0,2,1:T(4,128)(2,1)S(1)}, bf16[4,32,2,1792]{3,0,2,1:T(4,128)(2,1)}, u32[]{:S(2)}) copy-start(bf16[4,32,2,1792]{3,0,2,1:T(4,128)(2,1)} %copy.61) | copy-start | bytes 2752516
Sparse Core Ops, SparseCore 0:
  66.3 70.6 reduce-scatter.4
  159.8 46.0 reduce-scatter.2
  208.1 26.0 all-gather.4
  235.7 42.7 all-gather.2

commit v2 on v1

--- a/solution.py
+++ b/solution.py
@@ -20,7 +20,16 @@
 
 
 def exchange(parts, num_dp):
-    return lax.psum_scatter(parts, "dp", scatter_dimension=0, tiled=True)
+    rows, cols = parts.shape
+    parts = parts.reshape(num_dp, rows // num_dp, cols)
+    me = lax.axis_index("dp")
+    summed = lax.dynamic_index_in_dim(parts, me, 0, keepdims=False)
+    for shift in range(1, num_dp):
+        block = lax.dynamic_index_in_dim(parts, (me + shift) % num_dp, 0, keepdims=False)
+        pairs = [(i, (i + shift) % num_dp) for i in range(num_dp)]
+        came = lax.ppermute(block.astype(jnp.bfloat16), "dp", pairs)
+        summed = summed + came.astype(jnp.float32)
+    return summed
 
 
 def shards(

time: 340 us -> 279 us (0.82)
  blocking collectives: 148 us -> 36.2 us
  waiting for transfers between devices: 80.4 us -> 109 us
  starting transfers between devices: 6.14 us -> 30.7 us
  other arithmetic: 11 us -> 6.6 us
    all_to_all x2 -> x0, blocking collectives: 112 us -> none  [shards(): lax.all_to_all(flat_both, axes, split_axis=0, concat_axis=0, tiled=True)]
    ppermute x0 -> x6, waiting for transfers between devices: none -> 76.7 us  [exchange(): came = lax.ppermute(block.astype(jnp.bfloat16), 'dp', pairs)]
    reduce_scatter x2 -> x0, waiting for transfers between devices: 43.9 us -> none  [exchange(): return lax.psum_scatter(parts, 'dp', scatter_dimension=0, tiled=True)]
    all_gather x2, waiting for transfers between devices: 26 us -> 0.02 us  [shards(): lax.all_gather(jnp.concatenate([grad_pre, grad_lin, activated], axis=1),...]
    all_to_all x0 -> x2, waiting for transfers between devices: none -> 21.8 us  [shards(): lax.all_to_all(flat_both, axes, split_axis=0, concat_axis=0, tiled=True)]
    all_to_all x0 -> x2, starting transfers between devices: none -> 17.6 us  [shards(): lax.all_to_all(flat_both, axes, split_axis=0, concat_axis=0, tiled=True)]
    ppermute x0 -> x6, starting transfers between devices: none -> 7.1 us  [exchange(): came = lax.ppermute(block.astype(jnp.bfloat16), 'dp', pairs)]
    concatenate x2, other arithmetic: 4.46 us -> 0.73 us  [shards(): jnp.concatenate([gate_part, up_part, back_part], axis=1)]
  transfers between devices with their start and end apart: 5 -> 11, of which waited for: 3 -> 6; matrix products, arithmetic and copies ran while one was open for 16% -> 22% of each run, Pallas kernels for 0% -> 0%
where the time goes in v2:
time: 279 us; the launch traced here: 278 us
  waiting for transfers between devices  109 us (39%)
  matrix products  46.4 us (17%)
  blocking collectives  36.2 us (13%)
  local copies, waits for them, and re-layouts  34.2 us (12%)
  starting transfers between devices  30.7 us (11%)
  between operations  14.5 us (5%)
  other arithmetic  6.6 us (2%)
    ppermute x6, waiting for transfers between devices, exchange(): came = lax.ppermute(block.astype(jnp.bfloat16), 'dp', pairs)  76.7 us
    all_to_all x1, blocking collectives, shards(): lax.all_to_all(flat_back, axes, split_axis=0, concat_axis=0, tiled=True)  36.2 us
    all_to_all x2, waiting for transfers between devices, shards(): lax.all_to_all(flat_both, axes, split_axis=0, concat_axis=0, tiled=True)  21.8 us
    all_to_all x2, starting transfers between devices, shards(): lax.all_to_all(flat_both, axes, split_axis=0, concat_axis=0, tiled=True)  17.6 us
    dot_general x6, matrix products, contract_rows(): lax.dot_general(left, right, (((0,), (0,)), ((), ())), preferred_element_...  16.6 us
    all_to_all x1, waiting for transfers between devices, shards(): lax.all_to_all(flat_back, axes, split_axis=0, concat_axis=0, tiled=True)  10.5 us
    reshape x2, local copies, waits for them, and re-layouts, shards(): recv_both = recv_both.reshape(num_exp * num_dp * take, 2 * slice_width)  9.71 us
    dot_general x2, matrix products, shards(): up_part = jnp.dot(act_rows, up_local, preferred_element_type=jnp.float32)  7.62 us
  transfers between devices with their start and end apart: 11, of which 6 were waited for; matrix products, arithmetic and copies ran while one was open for 22% of the time, Pallas kernels for 0%

profile of v2, /device:TPU:1, one launch (start us, length us, event | category | flops | bytes accessed | tf_op | source)
XLA Modules:
  0.0 277.8 jit_solution(17111179940535311677)
XLA Ops:
  7.2 0.8 copy.51
  8.0 0.8 copy.57
  10.3 1.1 bitcast_bitcast_fusion
  12.1 1.6 reshape.97
  13.7 11.9 %all-to-all-start.2 = ((bf16[128,2,3584]{2,1,0:T(2,128)(2,1)}), bf16[128,2,3584]{2,1,0:T(2,128)(2,1)}, u32[]{:S(2)}, u32[]{:S(2)}) async-start(bf16[128,2,3584]{2,1,0:T(2,128)(2,1)} %reshape.97), calls=%async_computation.2 | async-start | bytes 3670016 | tf_op jit(solution)/shard_map/all_to_all | solution.py:83
  26.2 0.9 fusion
  27.1 4.0 %reshape.92 = bf16[128,3,3584]{2,1,0:T(4,128)(2,1)} reshape(bf16[4,96,3584]{2,1,0:T(8,128)(2,1)S(1)} %fusion) | data formatting | bytes 5505024 | tf_op jit(solution)/shard_map/reshape | solution.py:82
  31.1 21.8 %all-to-all-done.2 = bf16[128,2,3584]{2,1,0:T(2,128)(2,1)} async-done(((bf16[128,2,3584]{2,1,0:T(2,128)(2,1)}), bf16[128,2,3584]{2,1,0:T(2,128)(2,1)}, u32[]{:S(2)}, u32[]{:S(2)}) %all-to-all-start.2) | async-done | bytes 1835040 | tf_op jit(solution)/shard_map/all_to_all | solution.py:83
  53.0 5.7 %all-to-all-start = ((bf16[128,3,3584]{2,1,0:T(4,128)(2,1)}), bf16[128,3,3584]{2,1,0:T(4,128)(2,1)}, u32[]{:S(2)}, u32[]{:S(2)}) async-start(bf16[128,3,3584]{2,1,0:T(4,128)(2,1)} %reshape.92), calls=%async_computation | async-start | bytes 7340032 | tf_op jit(solution)/shard_map/all_to_all | solution.py:83
  58.7 4.1 %reshape.98 = bf16[256,3584]{1,0:T(8,128)(2,1)S(1)} reshape(bf16[128,2,3584]{2,1,0:T(2,128)(2,1)} %all-to-all-done.2) | data formatting | bytes 3670016 | tf_op jit(solution)/shard_map/reshape | solution.py:84
  62.8 3.8 %fusion.8 = f32[256,1024]{1,0:T(8,128)S(1)} fusion(bf16[1,1792,1024]{2,1,0:T(8,128)(2,1)} %param.12, bf16[256,3584]{1,0:T(8,128)(2,1)S(1)} %reshape.98), kind=kOutput, calls=%fused_computation.14 | convolution fusion | flops 939524096 | bytes 5636096 | tf_op jit(solution)/shard_map/dot_general | solution.py:88
  66.7 1.1 fusion.2
  67.8 0.9 copy-done.7
  68.7 1.1 fusion.16
  70.0 1.0 fusion.73
  71.1 1.4 collective-permute-start.3
  72.5 1.3 collective-permute-start.5
  73.8 1.7 collective-permute-start.4
  75.4 33.5 %collective-permute-done.3 = bf16[64,3072]{1,0:T(8,128)(2,1)} collective-permute-done((bf16[64,3072]{1,0:T(8,128)(2,1)}, bf16[64,3072]{1,0:T(8,128)(2,1)}, u32[]{:S(2)}, u32[]{:S(2)}) %collective-permute-start.3) | collective-permute-done | bytes 393248 | tf_op jit(solution)/shard_map/ppermute | solution.py:30
  108.9 8.5 %collective-permute-done.4 = bf16[64,3072]{1,0:T(8,128)(2,1)} collective-permute-done((bf16[64,3072]{1,0:T(8,128)(2,1)S(1)}, bf16[64,3072]{1,0:T(8,128)(2,1)}, u32[]{:S(2)}, u32[]{:S(2)}) %collective-permute-start.4) | collective-permute-done | bytes 393248 | tf_op jit(solution)/shard_map/ppermute | solution.py:30
  117.4 1.4 fusion.56
  119.0 0.8 pad_maximum_fusion.5
  120.0 5.6 %reshape.93 = bf16[384,3584]{1,0:T(8,128)(2,1)S(1)} reshape(bf16[128,3,3584]{2,1,0:T(4,128)(2,1)} %all-to-all-done) | data formatting | bytes 5505024 | tf_op jit(solution)/shard_map/reshape | solution.py:84
  125.7 3.8 %fusion.12 = f32[384,1024]{1,0:T(8,128)S(1)} fusion(bf16[1,1792,1024]{2,1,0:T(8,128)(2,1)} %param.12, bf16[384,3584]{1,0:T(8,128)(2,1)S(1)} %reshape.93), kind=kOutput, calls=%fused_computation.18 | convolution fusion | flops 1409286144 | bytes 6619136 | tf_op jit(solution)/shard_map/dot_general | solution.py:88
  129.5 1.6 fusion.4
  131.7 1.7 fusion.20
  134.5 2.4 collective-permute-start.2
  136.9 21.8 %collective-permute-done = bf16[96,3072]{1,0:T(8,128)(2,1)S(1)} collective-permute-done((bf16[96,3072]{1,0:T(8,128)(2,1)S(1)}, bf16[96,3072]{1,0:T(8,128)(2,1)S(1)}, u32[]{:S(2)}, u32[]{:S(2)}) %collective-permute-start) | collective-permute-done | bytes 589856 | tf_op jit(solution)/shard_map/ppermute | solution.py:30
  158.7 12.9 %collective-permute-done.1 = bf16[96,3072]{1,0:T(8,128)(2,1)S(1)} collective-permute-done((bf16[96,3072]{1,0:T(8,128)(2,1)S(1)}, bf16[96,3072]{1,0:T(8,128)(2,1)S(1)}, u32[]{:S(2)}, u32[]{:S(2)}) %collective-permute-start.1) | collective-permute-done | bytes 589856 | tf_op jit(solution)/shard_map/ppermute | solution.py:30
  172.1 0.9 pad_maximum_fusion.3
  173.1 3.5 %fusion.6 = f32[256,1792]{1,0:T(8,128)S(1)} fusion(bf16[1,1792,1024]{2,1,0:T(8,128)(2,1)} %param.12, bf16[256,3072]{1,0:T(8,128)(2,1)} %all-gather.5.cloned.1.call-done), kind=kOutput, calls=%fused_computation.12 | convolution fusion | flops 939524096 | bytes 6029312 | tf_op jit(solution)/shard_map/dot_general | solution.py:104
  176.6 3.1 %fusion.34 = bf16[256,1792]{1,0:T(8,128)(2,1)} fusion(f32[256,1792]{1,0:T(8,128)S(1)} %fusion.6, bf16[1,1792,1024]{2,1,0:T(8,128)(2,1)S(1)} %copy-done.9, bf16[256,3072]{1,0:T(8,128)(2,1)} %all-gather.5.cloned.1.call-done), kind=kOutput, calls=%fused_computation.35 | convolution fusion | flops 940441600 | bytes 6946816 | tf_op jit(solution)/shard_map/dot_general | solution.py:102
  179.7 3.1 %reshape.100 = bf16[128,2,1792]{2,1,0:T(2,128)(2,1)} reshape(bf16[256,1792]{1,0:T(8,128)(2,1)} %fusion.34) | data formatting | bytes 1835008 | tf_op jit(solution)/shard_map/reshape | solution.py:113
  182.8 36.2 %all_to_all.20 = bf16[128,2,1792]{2,1,0:T(2,128)(2,1)S(1)} all-to-all(bf16[128,2,1792]{2,1,0:T(2,128)(2,1)} %reshape.100), channel_id=1, replica_groups=mesh['expert'=32,'dp'=4] {'dp','expert'}, dimensions={0} | all-to-all | bytes 1835008 | tf_op jit(solution)/shard_map/all_to_all | solution.py:114
  219.0 1.7 copy.61
  220.8 4.1 %fusion.10 = f32[384,1792]{1,0:T(8,128)S(1)} fusion(bf16[1,1792,1024]{2,1,0:T(8,128)(2,1)} %param.12, bf16[384,3072]{1,0:T(8,128)(2,1)} %all-gather.3.cloned.1.call-done), kind=kOutput, calls=%fused_computation.16 | convolution fusion | flops 1409286144 | bytes 7208960 | tf_op jit(solution)/shard_map/dot_general | solution.py:104
  224.8 3.9 %fusion.28 = bf16[384,1792]{1,0:T(8,128)(2,1)} fusion(f32[384,1792]{1,0:T(8,128)S(1)} %fusion.10, bf16[1,1792,1024]{2,1,0:T(8,128)(2,1)S(1)} %copy-done.10, bf16[384,3072]{1,0:T(8,128)(2,1)} %all-gather.3.cloned.1.call-done), kind=kOutput, calls=%fused_computation.33 | convolution fusion | flops 1410662400 | bytes 8585216 | tf_op jit(solution)/shard_map/dot_general | solution.py:102
  228.7 3.8 %reshape.95 = bf16[128,3,1792]{2,1,0:T(4,128)(2,1)} reshape(bf16[384,1792]{1,0:T(8,128)(2,1)} %fusion.28) | data formatting | bytes 2752512 | tf_op jit(solution)/shard_map/reshape | solution.py:113
  232.5 5.8 %all-to-all-start.1 = ((bf16[128,3,1792]{2,1,0:T(4,128)(2,1)}), bf16[128,3,1792]{2,1,0:T(4,128)(2,1)}, u32[]{:S(2)}, u32[]{:S(2)}) async-start(bf16[128,3,1792]{2,1,0:T(4,128)(2,1)} %reshape.95), calls=%async_computation.1 | async-start | bytes 3670016 | tf_op jit(solution)/shard_map/all_to_all | solution.py:114
  238.3 3.4 %fusion.48 = f32[1792,1024]{1,0:T(8,128)S(1)} fusion(bf16[384,3584]{1,0:T(8,128)(2,1)S(1)} %reshape.93, bf16[384,3072]{1,0:T(8,128)(2,1)} %all-gather.3.cloned.1.call-done), kind=kOutput, calls=%fused_computation.51 | convolution fusion | flops 1409286144 | bytes 9502720 | tf_op jit(solution)/shard_map/dot_general | solution.py:17
  241.8 2.1 fusion.46
  243.9 3.0 %fusion.22 = bf16[1,1792,1024]{2,1,0:T(8,128)(2,1)} fusion(f32[1792,1024]{1,0:T(8,128)S(1)} %fusion.48, bf16[256,3584]{1,0:T(8,128)(2,1)S(1)} %copy-done.1, bf16[256,3072]{1,0:T(8,128)(2,1)S(1)} %copy-done.4), kind=kOutput, calls=%fused_computation.28 | convolution fusion | flops 943194112 | bytes 12451840 | tf_op jit(solution)/shard_map/dot_general | solution.py:17
  246.9 2.1 fusion.41
  249.0 3.0 %fusion.23 = bf16[1,1792,1024]{2,1,0:T(8,128)(2,1)} fusion(f32[1792,1024]{1,0:T(8,128)S(1)} %fusion.46, bf16[256,3584]{1,0:T(8,128)(2,1)S(1)} %copy-done.1, bf16[256,3072]{1,0:T(8,128)(2,1)S(1)} %copy-done.4), kind=kOutput, calls=%fused_computation.29 | convolution fusion | flops 943194112 | bytes 12451840 | tf_op jit(solution)/shard_map/dot_general | solution.py:17
  252.0 3.0 %fusion.24 = bf16[1,1024,1792]{2,1,0:T(8,128)(2,1)} fusion(f32[1024,1792]{1,0:T(8,128)S(1)} %fusion.41, bf16[256,3584]{1,0:T(8,128)(2,1)S(1)} %copy-done.1, bf16[256,3072]{1,0:T(8,128)(2,1)S(1)} %copy-done.4), kind=kOutput, calls=%fused_computation.30 | convolution fusion | flops 943194112 | bytes 12451840 | tf_op jit(solution)/shard_map/dot_general | solution.py:17
  255.1 10.5 %all-to-all-done.1 = bf16[128,3,1792]{2,1,0:T(4,128)(2,1)} async-done(((bf16[128,3,1792]{2,1,0:T(4,128)(2,1)}), bf16[128,3,1792]{2,1,0:T(4,128)(2,1)}, u32[]{:S(2)}, u32[]{:S(2)}) %all-to-all-start.1) | async-done | bytes 1376288 | tf_op jit(solution)/shard_map/all_to_all | solution.py:114
  265.6 2.8 %copy.60 = bf16[4,32,3,1792]{3,0,2,1:T(4,128)(2,1)S(1)} copy(bf16[4,32,3,1792]{3,2,1,0:T(4,128)(2,1)} %bitcast.11) | data formatting | bytes 2752512 | tf_op jit(solution)/shard_map/reshape | solution.py:115
  268.4 1.5 pad_maximum_fusion.2
  (65 shorter events, 6.8 us)
Async XLA Ops:
  13.7 39.2 %all-to-all-start.2 = ((bf16[128,2,3584]{2,1,0:T(2,128)(2,1)}), bf16[128,2,3584]{2,1,0:T(2,128)(2,1)}, u32[]{:S(2)}, u32[]{:S(2)}) async-start(bf16[128,2,3584]{2,1,0:T(2,128)(2,1)} %reshape.97), calls=%async_computation.2 | async-start | bytes 3670016 | tf_op jit(solution)/shard_map/all_to_all | solution.py:83
  53.0 67.1 %all-to-all-start = ((bf16[128,3,3584]{2,1,0:T(4,128)(2,1)}), bf16[128,3,3584]{2,1,0:T(4,128)(2,1)}, u32[]{:S(2)}, u32[]{:S(2)}) async-start(bf16[128,3,3584]{2,1,0:T(4,128)(2,1)} %reshape.92), calls=%async_computation | async-start | bytes 7340032 | tf_op jit(solution)/shard_map/all_to_all | solution.py:83
  58.7 114.4 %all-gather.5.cloned.1.call-start = ((), (), s32[]{:S(2)}) async-start(), calls=%async_computation.5 | async-start | bytes 1966080 | tf_op jit(solution)/shard_map/all_gather | solution.py:96
  62.8 5.0 %copy-start = (bf16[256,3584]{1,0:T(8,128)(2,1)}, bf16[256,3584]{1,0:T(8,128)(2,1)S(1)}, u32[]{:S(2)}) copy-start(bf16[256,3584]{1,0:T(8,128)(2,1)S(1)} %reshape.98) | copy-start | bytes 5505028
  62.8 3.9 %copy-start.5 = (bf16[1,1024,1792]{2,1,0:T(8,128)(2,1)S(1)}, bf16[1,1024,1792]{2,1,0:T(8,128)(2,1)}, u32[]{:S(2)}) copy-start(bf16[1,1024,1792]{2,1,0:T(8,128)(2,1)} %param.13) | copy-start | bytes 11010052
  66.7 2.0 copy-start.7
  71.1 37.8 %collective-permute-start.3 = (bf16[64,3072]{1,0:T(8,128)(2,1)}, bf16[64,3072]{1,0:T(8,128)(2,1)}, u32[]{:S(2)}, u32[]{:S(2)}) collective-permute-start(bf16[64,3072]{1,0:T(8,128)(2,1)} %get-tuple-element.7), channel_id=1, source_target_pairs={{0,1},{1,2},{2,3},{3,0},{4,5},{5,6},{6,7},{7,4},{8,9},{9,10},{10,1... | collective-permute-start | bytes 1179656 | tf_op jit(solution)/shard_map/ppermute | solution.py:30
  72.5 36.5 %collective-permute-start.5 = (bf16[64,3072]{1,0:T(8,128)(2,1)}, bf16[64,3072]{1,0:T(8,128)(2,1)}, u32[]{:S(2)}, u32[]{:S(2)}) collective-permute-start(bf16[64,3072]{1,0:T(8,128)(2,1)} %get-tuple-element.8), channel_id=1, source_target_pairs={{0,3},{1,0},{2,1},{3,2},{4,7},{5,4},{6,5},{7,6},{8,11},{9,8},{10,9... | collective-permute-start | bytes 1179656 | tf_op jit(solution)/shard_map/ppermute | solution.py:30
  73.8 43.7 %collective-permute-start.4 = (bf16[64,3072]{1,0:T(8,128)(2,1)S(1)}, bf16[64,3072]{1,0:T(8,128)(2,1)}, u32[]{:S(2)}, u32[]{:S(2)}) collective-permute-start(bf16[64,3072]{1,0:T(8,128)(2,1)S(1)} %get-tuple-element.9), channel_id=1, source_target_pairs={{0,2},{1,3},{2,0},{3,1},{4,6},{5,7},{6,4},{7,5},{8,10},{9,11},{10,... | collective-permute-start | bytes 1179656 | tf_op jit(solution)/shard_map/ppermute | solution.py:30
  119.8 101.0 %all-gather.3.cloned.1.call-start = ((), (), s32[]{:S(2)}) async-start(), calls=%async_computation.4 | async-start | bytes 2949120 | tf_op jit(solution)/shard_map/all_gather | solution.py:96
  125.7 3.8 %copy-start.6 = (bf16[1,1024,1792]{2,1,0:T(8,128)(2,1)S(1)}, bf16[1,1024,1792]{2,1,0:T(8,128)(2,1)}, u32[]{:S(2)}) copy-start(bf16[1,1024,1792]{2,1,0:T(8,128)(2,1)} %param.13) | copy-start | bytes 11010052
  129.5 2.2 copy-start.8
  134.2 24.5 %collective-permute-start = (bf16[96,3072]{1,0:T(8,128)(2,1)S(1)}, bf16[96,3072]{1,0:T(8,128)(2,1)S(1)}, u32[]{:S(2)}, u32[]{:S(2)}) collective-permute-start(bf16[96,3072]{1,0:T(8,128)(2,1)S(1)} %get-tuple-element.4), channel_id=1, source_target_pairs={{0,1},{1,2},{2,3},{3,0},{4,5},{5,6},{6,7},{7,4},{8,9},{9,10},{10,1... | collective-permute-start | bytes 1769480 | tf_op jit(solution)/shard_map/ppermute | solution.py:30
  134.5 24.1 %collective-permute-start.2 = (bf16[96,3072]{1,0:T(8,128)(2,1)S(1)}, bf16[96,3072]{1,0:T(8,128)(2,1)S(1)}, u32[]{:S(2)}, u32[]{:S(2)}) collective-permute-start(bf16[96,3072]{1,0:T(8,128)(2,1)S(1)} %get-tuple-element.5), channel_id=1, source_target_pairs={{0,3},{1,0},{2,1},{3,2},{4,7},{5,4},{6,5},{7,6},{8,11},{9,8},{10,9... | collective-permute-start | bytes 1769480 | tf_op jit(solution)/shard_map/ppermute | solution.py:30
  136.9 34.7 %collective-permute-start.1 = (bf16[96,3072]{1,0:T(8,128)(2,1)S(1)}, bf16[96,3072]{1,0:T(8,128)(2,1)S(1)}, u32[]{:S(2)}, u32[]{:S(2)}) collective-permute-start(bf16[96,3072]{1,0:T(8,128)(2,1)S(1)} %get-tuple-element.6), channel_id=1, source_target_pairs={{0,2},{1,3},{2,0},{3,1},{4,6},{5,7},{6,4},{7,5},{8,10},{9,11},{10,... | collective-permute-start | bytes 1769480 | tf_op jit(solution)/shard_map/ppermute | solution.py:30
  173.0 3.5 %copy-start.9 = (bf16[1,1792,1024]{2,1,0:T(8,128)(2,1)S(1)}, bf16[1,1792,1024]{2,1,0:T(8,128)(2,1)}, u32[]{:S(2)}) copy-start(bf16[1,1792,1024]{2,1,0:T(8,128)(2,1)} %param.11) | copy-start | bytes 11010052
  220.8 4.1 %copy-start.10 = (bf16[1,1792,1024]{2,1,0:T(8,128)(2,1)S(1)}, bf16[1,1792,1024]{2,1,0:T(8,128)(2,1)}, u32[]{:S(2)}) copy-start(bf16[1,1792,1024]{2,1,0:T(8,128)(2,1)} %param.11) | copy-start | bytes 11010052
  232.5 33.0 %all-to-all-start.1 = ((bf16[128,3,1792]{2,1,0:T(4,128)(2,1)}), bf16[128,3,1792]{2,1,0:T(4,128)(2,1)}, u32[]{:S(2)}, u32[]{:S(2)}) async-start(bf16[128,3,1792]{2,1,0:T(4,128)(2,1)} %reshape.95), calls=%async_computation.1 | async-start | bytes 3670016 | tf_op jit(solution)/shard_map/all_to_all | solution.py:114
  238.3 3.4 %copy-start.3 = (bf16[384,3072]{1,0:T(8,128)(2,1)S(1)}, bf16[384,3072]{1,0:T(8,128)(2,1)}, u32[]{:S(2)}) copy-start(bf16[384,3072]{1,0:T(8,128)(2,1)} %all-gather.3.cloned.1.call-done) | copy-start | bytes 7077892
  241.8 2.1 copy-start.1
  241.8 2.1 copy-start.4
  255.1 13.3 %copy-start.2 = (bf16[4,32,2,1792]{3,0,2,1:T(4,128)(2,1)S(1)}, bf16[4,32,2,1792]{3,0,2,1:T(4,128)(2,1)}, u32[]{:S(2)}) copy-start(bf16[4,32,2,1792]{3,0,2,1:T(4,128)(2,1)} %copy.61) | copy-start | bytes 2752516
Sparse Core Ops, SparseCore 0:
  119.9 33.8 all-gather.4
  173.1 42.3 all-gather.2

commit v3 on v2

--- a/solution.py
+++ b/solution.py
@@ -80,7 +80,10 @@
         )
         flat_both = (gathered_rows * weight[None]).astype(jnp.bfloat16)
         flat_both = flat_both.reshape(num_dp * num_exp, take, 2 * slice_width)
+        if pieces:
+            _, flat_both = lax.optimization_barrier((recv_prev, flat_both))
         recv_both = lax.all_to_all(flat_both, axes, split_axis=0, concat_axis=0, tiled=True)
+        recv_prev = recv_both
         recv_both = recv_both.reshape(num_exp * num_dp * take, 2 * slice_width)
         act_rows = recv_both[:, :slice_width]
         cot_rows = recv_both[:, slice_width:]

time: 279 us -> 301 us (1.079)
  blocking collectives: 36.2 us -> 0 us
  starting transfers between devices: 30.7 us -> 49 us
  matrix products: 46.4 us -> 62.1 us
  waiting for transfers between devices: 109 us -> 122 us
  local copies, waits for them, and re-layouts: 34.2 us -> 42 us
    ppermute x6, waiting for transfers between devices: 76.7 us -> 26.9 us  [exchange(): came = lax.ppermute(block.astype(jnp.bfloat16), 'dp', pairs)]
    all_to_all x2, waiting for transfers between devices: 21.8 us -> 64.9 us  [shards(): lax.all_to_all(flat_both, axes, split_axis=0, concat_axis=0, tiled=True)]
    all_to_all x1 -> x0, blocking collectives: 36.2 us -> none  [shards(): lax.all_to_all(flat_back, axes, split_axis=0, concat_axis=0, tiled=True)]
    all_to_all x1 -> x2, starting transfers between devices: 5.79 us -> 23.4 us  [shards(): lax.all_to_all(flat_back, axes, split_axis=0, concat_axis=0, tiled=True)]
    dot_general x6, matrix products: 16.6 us -> 31.3 us  [contract_rows(): lax.dot_general(left, right, (((0,), (0,)), ((), ())), preferred_element_...]
    all_gather x2, waiting for transfers between devices: 0.02 us -> 12.4 us  [shards(): lax.all_gather(jnp.concatenate([grad_pre, grad_lin, activated], axis=1),...]
    all_to_all x1 -> x2, waiting for transfers between devices: 10.5 us -> 17.6 us  [shards(): lax.all_to_all(flat_back, axes, split_axis=0, concat_axis=0, tiled=True)]
    reshape x2, local copies, waits for them, and re-layouts: 5.67 us -> 8.76 us  [shards(): flat_both = flat_both.reshape(num_dp * num_exp, take, 2 * slice_width)]
  transfers between devices with their start and end apart: 11 -> 12, of which waited for: 6 -> 8; matrix products, arithmetic and copies ran while one was open for 22% -> 23% of each run, Pallas kernels for 0% -> 0%
where the time goes in v3:
time: 301 us; the launch traced here: 297 us
  waiting for transfers between devices  122 us (41%)
  matrix products  62.1 us (21%)
  starting transfers between devices  49 us (16%)
  local copies, waits for them, and re-layouts  42 us (14%)
  between operations  14.7 us (5%)
  other arithmetic  7.26 us (2%)
    all_to_all x2, waiting for transfers between devices, shards(): lax.all_to_all(flat_both, axes, split_axis=0, concat_axis=0, tiled=True)  64.9 us
    dot_general x6, matrix products, contract_rows(): lax.dot_general(left, right, (((0,), (0,)), ((), ())), preferred_element_...  31.3 us
    ppermute x6, waiting for transfers between devices, exchange(): came = lax.ppermute(block.astype(jnp.bfloat16), 'dp', pairs)  26.9 us
    all_to_all x2, starting transfers between devices, shards(): lax.all_to_all(flat_back, axes, split_axis=0, concat_axis=0, tiled=True)  23.4 us
    all_to_all x2, starting transfers between devices, shards(): lax.all_to_all(flat_both, axes, split_axis=0, concat_axis=0, tiled=True)  18.6 us
    all_to_all x2, waiting for transfers between devices, shards(): lax.all_to_all(flat_back, axes, split_axis=0, concat_axis=0, tiled=True)  17.6 us
    all_gather x2, waiting for transfers between devices, shards(): lax.all_gather(jnp.concatenate([grad_pre, grad_lin, activated], axis=1),...  12.4 us
    reshape x2, local copies, waits for them, and re-layouts, shards(): recv_both = recv_both.reshape(num_exp * num_dp * take, 2 * slice_width)  10.6 us
  transfers between devices with their start and end apart: 12, of which 8 were waited for; matrix products, arithmetic and copies ran while one was open for 23% of the time, Pallas kernels for 0%

profile of v3, /device:TPU:1, one launch (start us, length us, event | category | flops | bytes accessed | tf_op | source)
XLA Modules:
  0.0 296.8 jit_solution(12731983063461410152)
XLA Ops:
  10.1 1.1 bitcast_bitcast_fusion
  11.4 0.9 fusion
  12.3 4.0 %reshape.92 = bf16[128,3,3584]{2,1,0:T(4,128)(2,1)} reshape(bf16[4,96,3584]{2,1,0:T(8,128)(2,1)S(1)} %fusion) | data formatting | bytes 5505024 | tf_op jit(solution)/shard_map/reshape | solution.py:82
  16.4 11.9 %all-to-all-start = ((bf16[128,3,3584]{2,1,0:T(4,128)(2,1)}), bf16[128,3,3584]{2,1,0:T(4,128)(2,1)}, u32[]{:S(2)}, u32[]{:S(2)}) async-start(bf16[128,3,3584]{2,1,0:T(4,128)(2,1)} %reshape.92), calls=%async_computation | async-start | bytes 7340032 | tf_op jit(solution)/shard_map/all_to_all | solution.py:85
  28.7 1.0 concatenate.28
  29.7 45.7 %all-to-all-done = bf16[128,3,3584]{2,1,0:T(4,128)(2,1)} async-done(((bf16[128,3,3584]{2,1,0:T(4,128)(2,1)}), bf16[128,3,3584]{2,1,0:T(4,128)(2,1)}, u32[]{:S(2)}, u32[]{:S(2)}) %all-to-all-start) | async-done | bytes 2752544 | tf_op jit(solution)/shard_map/all_to_all | solution.py:85
  75.4 5.6 %reshape.93 = bf16[384,3584]{1,0:T(8,128)(2,1)S(1)} reshape(bf16[128,3,3584]{2,1,0:T(4,128)(2,1)} %all-to-all-done) | data formatting | bytes 5505024 | tf_op jit(solution)/shard_map/reshape | solution.py:87
  81.0 3.8 %fusion.12 = f32[384,1024]{1,0:T(8,128)S(1)} fusion(bf16[1,1792,1024]{2,1,0:T(8,128)(2,1)} %param.12, bf16[384,3584]{1,0:T(8,128)(2,1)S(1)} %reshape.93), kind=kOutput, calls=%fused_computation.18 | convolution fusion | flops 1409286144 | bytes 6619136 | tf_op jit(solution)/shard_map/dot_general | solution.py:91
  84.8 1.6 fusion.4
  86.9 1.7 fusion.20
  89.1 2.1 copy-done
  91.2 1.3 fusion.65
  92.6 2.5 collective-permute-start.2
  95.2 1.9 fusion.1
  97.1 4.7 %reshape.97 = bf16[128,2,3584]{2,1,0:T(2,128)(2,1)} reshape(bf16[4,64,3584]{2,1,0:T(8,128)(2,1)} %fusion.1) | data formatting | bytes 3670016 | tf_op jit(solution)/shard_map/reshape | solution.py:82
  101.8 6.7 %all-to-all-start.2 = ((bf16[128,2,3584]{2,1,0:T(2,128)(2,1)}), bf16[128,2,3584]{2,1,0:T(2,128)(2,1)}, u32[]{:S(2)}, u32[]{:S(2)}) async-start(bf16[128,2,3584]{2,1,0:T(2,128)(2,1)} %reshape.97), calls=%async_computation.2 | async-start | bytes 3670016 | tf_op jit(solution)/shard_map/all_to_all | solution.py:85
  108.6 11.0 %collective-permute-done.1 = bf16[96,3072]{1,0:T(8,128)(2,1)} collective-permute-done((bf16[96,3072]{1,0:T(8,128)(2,1)}, bf16[96,3072]{1,0:T(8,128)(2,1)}, u32[]{:S(2)}, u32[]{:S(2)}) %collective-permute-start.1) | collective-permute-done | bytes 589856 | tf_op jit(solution)/shard_map/ppermute | solution.py:30
  119.6 2.1 fusion.45
  123.1 19.2 %all-to-all-done.2 = bf16[128,2,3584]{2,1,0:T(2,128)(2,1)} async-done(((bf16[128,2,3584]{2,1,0:T(2,128)(2,1)}), bf16[128,2,3584]{2,1,0:T(2,128)(2,1)}, u32[]{:S(2)}, u32[]{:S(2)}) %all-to-all-start.2) | async-done | bytes 1835040 | tf_op jit(solution)/shard_map/all_to_all | solution.py:85
  142.3 4.9 %reshape.98 = bf16[256,3584]{1,0:T(8,128)(2,1)} reshape(bf16[128,2,3584]{2,1,0:T(2,128)(2,1)} %all-to-all-done.2) | data formatting | bytes 3670016 | tf_op jit(solution)/shard_map/reshape | solution.py:87
  147.2 3.6 %fusion.8 = f32[256,1024]{1,0:T(8,128)S(1)} fusion(bf16[1,1792,1024]{2,1,0:T(8,128)(2,1)} %param.12, bf16[256,3584]{1,0:T(8,128)(2,1)} %reshape.98), kind=kOutput, calls=%fused_computation.14 | convolution fusion | flops 939524096 | bytes 5636096 | tf_op jit(solution)/shard_map/dot_general | solution.py:91
  151.3 1.1 fusion.2
  152.4 0.9 copy-done.8
  153.4 1.2 fusion.16
  155.8 2.1 collective-permute-start.5
  157.9 1.1 collective-permute-start.4
  159.0 8.3 %collective-permute-done.3 = bf16[64,3072]{1,0:T(8,128)(2,1)S(1)} collective-permute-done((bf16[64,3072]{1,0:T(8,128)(2,1)S(1)}, bf16[64,3072]{1,0:T(8,128)(2,1)S(1)}, u32[]{:S(2)}, u32[]{:S(2)}) %collective-permute-start.3) | collective-permute-done | bytes 393248 | tf_op jit(solution)/shard_map/ppermute | solution.py:30
  167.3 7.6 %collective-permute-done.4 = bf16[64,3072]{1,0:T(8,128)(2,1)S(1)} collective-permute-done((bf16[64,3072]{1,0:T(8,128)(2,1)S(1)}, bf16[64,3072]{1,0:T(8,128)(2,1)S(1)}, u32[]{:S(2)}, u32[]{:S(2)}) %collective-permute-start.4) | collective-permute-done | bytes 393248 | tf_op jit(solution)/shard_map/ppermute | solution.py:30
  176.1 4.1 %fusion.10 = f32[384,1792]{1,0:T(8,128)S(1)} fusion(bf16[1,1792,1024]{2,1,0:T(8,128)(2,1)} %param.12, bf16[384,3072]{1,0:T(8,128)(2,1)} %all-gather.3.cloned.1.call-done), kind=kOutput, calls=%fused_computation.16 | convolution fusion | flops 1409286144 | bytes 7208960 | tf_op jit(solution)/shard_map/dot_general | solution.py:107
  180.2 3.9 %fusion.28 = bf16[384,1792]{1,0:T(8,128)(2,1)} fusion(f32[384,1792]{1,0:T(8,128)S(1)} %fusion.10, bf16[1,1792,1024]{2,1,0:T(8,128)(2,1)S(1)} %copy-done.9, bf16[384,3072]{1,0:T(8,128)(2,1)} %all-gather.3.cloned.1.call-done), kind=kOutput, calls=%fused_computation.33 | convolution fusion | flops 1410662400 | bytes 8585216 | tf_op jit(solution)/shard_map/dot_general | solution.py:105
  184.0 3.9 %reshape.95 = bf16[128,3,1792]{2,1,0:T(4,128)(2,1)} reshape(bf16[384,1792]{1,0:T(8,128)(2,1)} %fusion.28) | data formatting | bytes 2752512 | tf_op jit(solution)/shard_map/reshape | solution.py:116
  187.9 6.2 %fusion.48 = f32[1792,1024]{1,0:T(8,128)} fusion(bf16[384,3584]{1,0:T(8,128)(2,1)S(1)} %reshape.93, bf16[384,3072]{1,0:T(8,128)(2,1)} %all-gather.3.cloned.1.call-done), kind=kOutput, calls=%fused_computation.51 | convolution fusion | flops 1409286144 | bytes 9502720 | tf_op jit(solution)/shard_map/dot_general | solution.py:17
  194.1 12.4 %all-gather.5.cloned.1.call-done = bf16[256,3072]{1,0:T(8,128)(2,1)} async-done(((bf16[64,3072]{1,0:T(8,128)(2,1)}), bf16[256,3072]{1,0:T(8,128)(2,1)}) %all-gather.5.cloned.1.call-update) | async-done | bytes 1572880 | tf_op jit(solution)/shard_map/all_gather | solution.py:99
  206.5 3.5 %fusion.6 = f32[256,1792]{1,0:T(8,128)S(1)} fusion(bf16[1,1792,1024]{2,1,0:T(8,128)(2,1)} %param.12, bf16[256,3072]{1,0:T(8,128)(2,1)} %all-gather.5.cloned.1.call-done), kind=kOutput, calls=%fused_computation.12 | convolution fusion | flops 939524096 | bytes 6029312 | tf_op jit(solution)/shard_map/dot_general | solution.py:107
  210.0 3.1 %fusion.34 = bf16[256,1792]{1,0:T(8,128)(2,1)} fusion(f32[256,1792]{1,0:T(8,128)S(1)} %fusion.6, bf16[1,1792,1024]{2,1,0:T(8,128)(2,1)S(1)} %copy-done.10, bf16[256,3072]{1,0:T(8,128)(2,1)} %all-gather.5.cloned.1.call-done), kind=kOutput, calls=%fused_computation.35 | convolution fusion | flops 940441600 | bytes 6946816 | tf_op jit(solution)/shard_map/dot_general | solution.py:105
  213.1 3.1 %reshape.100 = bf16[128,2,1792]{2,1,0:T(2,128)(2,1)} reshape(bf16[256,1792]{1,0:T(8,128)(2,1)} %fusion.34) | data formatting | bytes 1835008 | tf_op jit(solution)/shard_map/reshape | solution.py:116
  216.2 17.4 %all-to-all-start.3 = ((bf16[128,2,1792]{2,1,0:T(2,128)(2,1)}), bf16[128,2,1792]{2,1,0:T(2,128)(2,1)}, u32[]{:S(2)}, u32[]{:S(2)}) async-start(bf16[128,2,1792]{2,1,0:T(2,128)(2,1)} %reshape.100), calls=%async_computation.3 | async-start | bytes 1835008 | tf_op jit(solution)/shard_map/all_to_all | solution.py:117
  233.6 6.2 %fusion.46 = f32[1792,1024]{1,0:T(8,128)} fusion(bf16[384,3584]{1,0:T(8,128)(2,1)S(1)} %reshape.93, bf16[384,3072]{1,0:T(8,128)(2,1)} %all-gather.3.cloned.1.call-done), kind=kOutput, calls=%fused_computation.49 | convolution fusion | flops 1409286144 | bytes 9502720 | tf_op jit(solution)/shard_map/dot_general | solution.py:17
  239.8 6.2 %fusion.41 = f32[1024,1792]{1,0:T(8,128)} fusion(bf16[384,3584]{1,0:T(8,128)(2,1)S(1)} %reshape.93, bf16[384,3072]{1,0:T(8,128)(2,1)} %all-gather.3.cloned.1.call-done), kind=kOutput, calls=%fused_computation.40 | convolution fusion | flops 1409286144 | bytes 9502720 | tf_op jit(solution)/shard_map/dot_general | solution.py:17
  246.1 4.9 %all-to-all-done.3 = bf16[128,2,1792]{2,1,0:T(2,128)(2,1)} async-done(((bf16[128,2,1792]{2,1,0:T(2,128)(2,1)}), bf16[128,2,1792]{2,1,0:T(2,128)(2,1)}, u32[]{:S(2)}, u32[]{:S(2)}) %all-to-all-start.3) | async-done | bytes 917536 | tf_op jit(solution)/shard_map/all_to_all | solution.py:117
  251.0 5.9 %all-to-all-start.1 = ((bf16[128,3,1792]{2,1,0:T(4,128)(2,1)}), bf16[128,3,1792]{2,1,0:T(4,128)(2,1)}, u32[]{:S(2)}, u32[]{:S(2)}) async-start(bf16[128,3,1792]{2,1,0:T(4,128)(2,1)} %reshape.95), calls=%async_computation.1 | async-start | bytes 3670016 | tf_op jit(solution)/shard_map/all_to_all | solution.py:117
  257.0 6.7 %fusion.22 = bf16[1,1792,1024]{2,1,0:T(8,128)(2,1)} fusion(f32[1792,1024]{1,0:T(8,128)} %fusion.48, bf16[256,3584]{1,0:T(8,128)(2,1)} %reshape.98, bf16[256,3072]{1,0:T(8,128)(2,1)} %all-gather.5.cloned.1.call-done), kind=kOutput, calls=%fused_computation.28 | convolution fusion | flops 943194112 | bytes 12451840 | tf_op jit(solution)/shard_map/dot_general | solution.py:17
  263.7 3.0 %fusion.23 = bf16[1,1792,1024]{2,1,0:T(8,128)(2,1)} fusion(f32[1792,1024]{1,0:T(8,128)S(1)} %bitcast.85, bf16[256,3584]{1,0:T(8,128)(2,1)S(1)} %copy-done.2, bf16[256,3072]{1,0:T(8,128)(2,1)S(1)} %copy-done.4), kind=kOutput, calls=%fused_computation.29 | convolution fusion | flops 943194112 | bytes 12451840 | tf_op jit(solution)/shard_map/dot_general | solution.py:17
  266.8 3.0 %fusion.24 = bf16[1,1024,1792]{2,1,0:T(8,128)(2,1)} fusion(f32[1024,1792]{1,0:T(8,128)S(1)} %bitcast.87, bf16[256,3584]{1,0:T(8,128)(2,1)S(1)} %copy-done.2, bf16[256,3072]{1,0:T(8,128)(2,1)S(1)} %copy-done.4), kind=kOutput, calls=%fused_computation.30 | convolution fusion | flops 943194112 | bytes 12451840 | tf_op jit(solution)/shard_map/dot_general | solution.py:17
  269.8 1.9 copy.61
  271.7 12.7 %all-to-all-done.1 = bf16[128,3,1792]{2,1,0:T(4,128)(2,1)} async-done(((bf16[128,3,1792]{2,1,0:T(4,128)(2,1)}), bf16[128,3,1792]{2,1,0:T(4,128)(2,1)}, u32[]{:S(2)}, u32[]{:S(2)}) %all-to-all-start.1) | async-done | bytes 1376288 | tf_op jit(solution)/shard_map/all_to_all | solution.py:117
  284.4 2.8 copy.60
  287.2 1.5 pad_maximum_fusion.2
  (76 shorter events, 10.1 us)
Async XLA Ops:
  16.4 59.0 %all-to-all-start = ((bf16[128,3,3584]{2,1,0:T(4,128)(2,1)}), bf16[128,3,3584]{2,1,0:T(4,128)(2,1)}, u32[]{:S(2)}, u32[]{:S(2)}) async-start(bf16[128,3,3584]{2,1,0:T(4,128)(2,1)} %reshape.92), calls=%async_computation | async-start | bytes 7340032 | tf_op jit(solution)/shard_map/all_to_all | solution.py:85
  81.0 3.8 %copy-start.5 = (bf16[1,1024,1792]{2,1,0:T(8,128)(2,1)S(1)}, bf16[1,1024,1792]{2,1,0:T(8,128)(2,1)}, u32[]{:S(2)}) copy-start(bf16[1,1024,1792]{2,1,0:T(8,128)(2,1)} %param.13) | copy-start | bytes 11010052
  84.8 2.0 copy-start.7
  89.1 2.2 copy-start
  89.1 6.1 %copy-start.3 = (f32[64,3584]{1,0:T(8,128)S(1)}, f32[64,3584]{1,0:T(8,128)}, u32[]{:S(2)}) copy-start(f32[64,3584]{1,0:T(8,128)} %concatenate.28) | copy-start | bytes 2752516
  92.5 16.1 %collective-permute-start = (bf16[96,3072]{1,0:T(8,128)(2,1)}, bf16[96,3072]{1,0:T(8,128)(2,1)}, u32[]{:S(2)}, u32[]{:S(2)}) collective-permute-start(bf16[96,3072]{1,0:T(8,128)(2,1)} %get-tuple-element.6), channel_id=1, source_target_pairs={{0,1},{1,2},{2,3},{3,0},{4,5},{5,6},{6,7},{7,4},{8,9},{9,10},{10,1... | collective-permute-start | bytes 1769480 | tf_op jit(solution)/shard_map/ppermute | solution.py:30
  92.6 16.0 %collective-permute-start.2 = (bf16[96,3072]{1,0:T(8,128)(2,1)}, bf16[96,3072]{1,0:T(8,128)(2,1)}, u32[]{:S(2)}, u32[]{:S(2)}) collective-permute-start(bf16[96,3072]{1,0:T(8,128)(2,1)} %get-tuple-element.7), channel_id=1, source_target_pairs={{0,3},{1,0},{2,1},{3,2},{4,7},{5,4},{6,5},{7,6},{8,11},{9,8},{10,9... | collective-permute-start | bytes 1769480 | tf_op jit(solution)/shard_map/ppermute | solution.py:30
  95.1 24.5 %collective-permute-start.1 = (bf16[96,3072]{1,0:T(8,128)(2,1)}, bf16[96,3072]{1,0:T(8,128)(2,1)}, u32[]{:S(2)}, u32[]{:S(2)}) collective-permute-start(bf16[96,3072]{1,0:T(8,128)(2,1)} %get-tuple-element.8), channel_id=1, source_target_pairs={{0,2},{1,3},{2,0},{3,1},{4,6},{5,7},{6,4},{7,5},{8,10},{9,11},{10,... | collective-permute-start | bytes 1769480 | tf_op jit(solution)/shard_map/ppermute | solution.py:30
  101.8 40.5 %all-to-all-start.2 = ((bf16[128,2,3584]{2,1,0:T(2,128)(2,1)}), bf16[128,2,3584]{2,1,0:T(2,128)(2,1)}, u32[]{:S(2)}, u32[]{:S(2)}) async-start(bf16[128,2,3584]{2,1,0:T(2,128)(2,1)} %reshape.97), calls=%async_computation.2 | async-start | bytes 3670016 | tf_op jit(solution)/shard_map/all_to_all | solution.py:85
  108.6 67.5 %all-gather.3.cloned.1.call-start = ((), (), s32[]{:S(2)}) async-start(), calls=%async_computation.4 | async-start | bytes 2949120 | tf_op jit(solution)/shard_map/all_gather | solution.py:99
  122.8 83.7 %all-gather.5.cloned.1.call-start = ((), (), s32[]{:S(2)}) async-start(), calls=%async_computation.5 | async-start | bytes 1966080 | tf_op jit(solution)/shard_map/all_gather | solution.py:99
  147.2 3.6 %copy-start.1 = (bf16[256,3584]{1,0:T(8,128)(2,1)S(1)}, bf16[256,3584]{1,0:T(8,128)(2,1)}, u32[]{:S(2)}) copy-start(bf16[256,3584]{1,0:T(8,128)(2,1)} %reshape.98) | copy-start | bytes 5505028
  147.2 4.1 %copy-start.6 = (bf16[1,1024,1792]{2,1,0:T(8,128)(2,1)S(1)}, bf16[1,1024,1792]{2,1,0:T(8,128)(2,1)}, u32[]{:S(2)}) copy-start(bf16[1,1024,1792]{2,1,0:T(8,128)(2,1)} %param.13) | copy-start | bytes 11010052
  151.3 2.1 copy-start.8
  155.1 12.2 %collective-permute-start.3 = (bf16[64,3072]{1,0:T(8,128)(2,1)S(1)}, bf16[64,3072]{1,0:T(8,128)(2,1)S(1)}, u32[]{:S(2)}, u32[]{:S(2)}) collective-permute-start(bf16[64,3072]{1,0:T(8,128)(2,1)S(1)} %get-tuple-element.9), channel_id=1, source_target_pairs={{0,1},{1,2},{2,3},{3,0},{4,5},{5,6},{6,7},{7,4},{8,9},{9,10},{10,1... | collective-permute-start | bytes 1179656 | tf_op jit(solution)/shard_map/ppermute | solution.py:30
  155.8 11.5 %collective-permute-start.5 = (bf16[64,3072]{1,0:T(8,128)(2,1)S(1)}, bf16[64,3072]{1,0:T(8,128)(2,1)S(1)}, u32[]{:S(2)}, u32[]{:S(2)}) collective-permute-start(bf16[64,3072]{1,0:T(8,128)(2,1)S(1)} %get-tuple-element.10), channel_id=1, source_target_pairs={{0,3},{1,0},{2,1},{3,2},{4,7},{5,4},{6,5},{7,6},{8,11},{9,8},{10,9... | collective-permute-start | bytes 1179656 | tf_op jit(solution)/shard_map/ppermute | solution.py:30
  157.9 17.0 %collective-permute-start.4 = (bf16[64,3072]{1,0:T(8,128)(2,1)S(1)}, bf16[64,3072]{1,0:T(8,128)(2,1)S(1)}, u32[]{:S(2)}, u32[]{:S(2)}) collective-permute-start(bf16[64,3072]{1,0:T(8,128)(2,1)S(1)} %get-tuple-element.11), channel_id=1, source_target_pairs={{0,2},{1,3},{2,0},{3,1},{4,6},{5,7},{6,4},{7,5},{8,10},{9,11},{10,... | collective-permute-start | bytes 1179656 | tf_op jit(solution)/shard_map/ppermute | solution.py:30
  176.1 4.1 %copy-start.9 = (bf16[1,1792,1024]{2,1,0:T(8,128)(2,1)S(1)}, bf16[1,1792,1024]{2,1,0:T(8,128)(2,1)}, u32[]{:S(2)}) copy-start(bf16[1,1792,1024]{2,1,0:T(8,128)(2,1)} %param.11) | copy-start | bytes 11010052
  206.5 3.5 %copy-start.10 = (bf16[1,1792,1024]{2,1,0:T(8,128)(2,1)S(1)}, bf16[1,1792,1024]{2,1,0:T(8,128)(2,1)}, u32[]{:S(2)}) copy-start(bf16[1,1792,1024]{2,1,0:T(8,128)(2,1)} %param.11) | copy-start | bytes 11010052
  216.2 34.8 %all-to-all-start.3 = ((bf16[128,2,1792]{2,1,0:T(2,128)(2,1)}), bf16[128,2,1792]{2,1,0:T(2,128)(2,1)}, u32[]{:S(2)}, u32[]{:S(2)}) async-start(bf16[128,2,1792]{2,1,0:T(2,128)(2,1)} %reshape.100), calls=%async_computation.3 | async-start | bytes 1835008 | tf_op jit(solution)/shard_map/all_to_all | solution.py:117
  251.0 12.7 %slice-start = ((s8[7340032]{0:T(1024)(128)(4,1)}), s8[3145728]{0:T(1024)(128)(4,1)S(1)}, s32[]{:S(2)}) async-start(s8[7340032]{0:T(1024)(128)(4,1)} %bitcast.84), calls=%async_computation.6 | async-start | bytes 6291456
  251.0 33.4 %all-to-all-start.1 = ((bf16[128,3,1792]{2,1,0:T(4,128)(2,1)}), bf16[128,3,1792]{2,1,0:T(4,128)(2,1)}, u32[]{:S(2)}, u32[]{:S(2)}) async-start(bf16[128,3,1792]{2,1,0:T(4,128)(2,1)} %reshape.95), calls=%async_computation.1 | async-start | bytes 3670016 | tf_op jit(solution)/shard_map/all_to_all | solution.py:117
  256.9 6.7 %slice-start.1 = ((s8[7340032]{0:T(1024)(128)(4,1)}), s8[4194304]{0:T(1024)(128)(4,1)S(1)}, s32[]{:S(2)}) async-start(s8[7340032]{0:T(1024)(128)(4,1)} %bitcast.84), calls=%async_computation.7 | async-start | bytes 8388608
  256.9 6.7 %copy-start.2 = (bf16[256,3584]{1,0:T(8,128)(2,1)S(1)}, bf16[256,3584]{1,0:T(8,128)(2,1)}, u32[]{:S(2)}) copy-start(bf16[256,3584]{1,0:T(8,128)(2,1)} %reshape.98) | copy-start | bytes 5505028
  257.0 6.7 %copy-start.4 = (bf16[256,3072]{1,0:T(8,128)(2,1)S(1)}, bf16[256,3072]{1,0:T(8,128)(2,1)}, u32[]{:S(2)}) copy-start(bf16[256,3072]{1,0:T(8,128)(2,1)} %all-gather.5.cloned.1.call-done) | copy-start | bytes 4718596
  257.0 9.8 %slice-start.2 = ((s8[7340032]{0:T(1024)(128)(4,1)}), s8[4194304]{0:T(1024)(128)(4,1)S(1)}, s32[]{:S(2)}) async-start(s8[7340032]{0:T(1024)(128)(4,1)} %bitcast.86), calls=%async_computation.8 | async-start | bytes 8388608
  263.7 3.1 %slice-start.3 = ((s8[7340032]{0:T(1024)(128)(4,1)}), s8[3145728]{0:T(1024)(128)(4,1)S(1)}, s32[]{:S(2)}) async-start(s8[7340032]{0:T(1024)(128)(4,1)} %bitcast.86), calls=%async_computation.9 | async-start | bytes 6291456
Sparse Core Ops, SparseCore 0:
  122.9 38.3 all-gather.2
  176.2 30.2 all-gather.4

commit v4 on v2

--- a/solution.py
+++ b/solution.py
@@ -17,6 +17,18 @@
     return lax.dot_general(
         left, right, (((0,), (0,)), ((), ())), preferred_element_type=jnp.float32
     )
+
+
+def exchange_queued(parts, num_dp):
+    rows, cols = parts.shape
+    parts = parts.reshape(num_dp, rows // num_dp, cols)
+    me = lax.axis_index("dp")
+    own = lax.dynamic_index_in_dim(parts, me, 0, keepdims=False)
+    came = lax.all_to_all(
+        parts.astype(jnp.bfloat16), "dp", split_axis=0, concat_axis=0, tiled=True
+    )
+    others = (jnp.arange(num_dp, dtype=jnp.int32) != me).astype(jnp.float32)
+    return own + jnp.sum(came.astype(jnp.float32) * others[:, None, None], axis=0)
 
 
 def exchange(parts, num_dp):
@@ -89,7 +101,8 @@
         back_part = lax.dot_general(
             cot_rows, down_local, (((1,), (1,)), ((), ())), preferred_element_type=jnp.float32
         )
-        summed = exchange(jnp.concatenate([gate_part, up_part, back_part], axis=1), num_dp)
+        swap = exchange if lo == 0 else exchange_queued
+        summed = swap(jnp.concatenate([gate_part, up_part, back_part], axis=1), num_dp)
         grad_pre, grad_lin, activated = swiglu_back(
             summed[:, :hidden], summed[:, hidden : 2 * hidden], summed[:, 2 * hidden :]
         )

time: 279 us -> 283 us (1.014)
  other arithmetic: 6.6 us -> 12 us
  matrix products: 46.4 us -> 49.9 us
  waiting for transfers between devices: 109 us -> 106 us
    ppermute x6 -> x3, waiting for transfers between devices: 76.7 us -> 36.1 us  [exchange(): came = lax.ppermute(block.astype(jnp.bfloat16), 'dp', pairs)]
    all_to_all x2, waiting for transfers between devices: 21.8 us -> 54.5 us  [shards(): lax.all_to_all(flat_both, axes, split_axis=0, concat_axis=0, tiled=True)]
    all_to_all x0 -> x1, starting transfers between devices: none -> 4.36 us  [exchange_queued(): lax.all_to_all(parts.astype(jnp.bfloat16), 'dp', split_axis=0, concat_axi...]
    ppermute x6 -> x3, starting transfers between devices: 7.1 us -> 2.75 us  [exchange(): came = lax.ppermute(block.astype(jnp.bfloat16), 'dp', pairs)]
    all_to_all x0 -> x1, waiting for transfers between devices: none -> 3.34 us  [exchange_queued(): lax.all_to_all(parts.astype(jnp.bfloat16), 'dp', split_axis=0, concat_axi...]
  transfers between devices with their start and end apart: 11 -> 9, of which waited for: 6 -> 8; matrix products, arithmetic and copies ran while one was open for 22% -> 23% of each run, Pallas kernels for 0% -> 0%
where the time goes in v4:
time: 283 us; the launch traced here: 282 us
  waiting for transfers between devices  106 us (37%)
  matrix products  49.9 us (18%)
  blocking collectives  34.5 us (12%)
  local copies, waits for them, and re-layouts  34.3 us (12%)
  starting transfers between devices  30.8 us (11%)
  between operations  14.5 us (5%)
  other arithmetic  12 us (4%)
    all_to_all x2, waiting for transfers between devices, shards(): lax.all_to_all(flat_both, axes, split_axis=0, concat_axis=0, tiled=True)  54.5 us
    ppermute x3, waiting for transfers between devices, exchange(): came = lax.ppermute(block.astype(jnp.bfloat16), 'dp', pairs)  36.1 us
    all_to_all x1, blocking collectives, shards(): lax.all_to_all(flat_back, axes, split_axis=0, concat_axis=0, tiled=True)  34.5 us
    all_to_all x2, starting transfers between devices, shards(): lax.all_to_all(flat_both, axes, split_axis=0, concat_axis=0, tiled=True)  17.6 us
    dot_general x6, matrix products, contract_rows(): lax.dot_general(left, right, (((0,), (0,)), ((), ())), preferred_element_...  16.6 us
    all_to_all x1, waiting for transfers between devices, shards(): lax.all_to_all(flat_back, axes, split_axis=0, concat_axis=0, tiled=True)  10.5 us
    reshape x2, local copies, waits for them, and re-layouts, shards(): recv_both = recv_both.reshape(num_exp * num_dp * take, 2 * slice_width)  9.71 us
    dot_general x2, matrix products, shards(): up_part = jnp.dot(act_rows, up_local, preferred_element_type=jnp.float32)  8.8 us
  transfers between devices with their start and end apart: 9, of which 8 were waited for; matrix products, arithmetic and copies ran while one was open for 23% of the time, Pallas kernels for 0%

profile of v4, /device:TPU:1, one launch (start us, length us, event | category | flops | bytes accessed | tf_op | source)
XLA Modules:
  0.0 282.2 jit_solution(11683774309585950573)
XLA Ops:
  10.3 1.1 bitcast_bitcast_fusion
  12.1 1.6 reshape.99
  13.7 11.9 %all-to-all-start.2 = ((bf16[128,2,3584]{2,1,0:T(2,128)(2,1)}), bf16[128,2,3584]{2,1,0:T(2,128)(2,1)}, u32[]{:S(2)}, u32[]{:S(2)}) async-start(bf16[128,2,3584]{2,1,0:T(2,128)(2,1)} %reshape.99), calls=%async_computation.2 | async-start | bytes 3670016 | tf_op jit(solution)/shard_map/all_to_all | solution.py:95
  26.1 0.9 fusion
  27.0 4.0 %reshape.94 = bf16[128,3,3584]{2,1,0:T(4,128)(2,1)} reshape(bf16[4,96,3584]{2,1,0:T(8,128)(2,1)S(1)} %fusion) | data formatting | bytes 5505024 | tf_op jit(solution)/shard_map/reshape | solution.py:94
  31.1 21.9 %all-to-all-done.2 = bf16[128,2,3584]{2,1,0:T(2,128)(2,1)} async-done(((bf16[128,2,3584]{2,1,0:T(2,128)(2,1)}), bf16[128,2,3584]{2,1,0:T(2,128)(2,1)}, u32[]{:S(2)}, u32[]{:S(2)}) %all-to-all-start.2) | async-done | bytes 1835040 | tf_op jit(solution)/shard_map/all_to_all | solution.py:95
  53.0 5.7 %all-to-all-start = ((bf16[128,3,3584]{2,1,0:T(4,128)(2,1)}), bf16[128,3,3584]{2,1,0:T(4,128)(2,1)}, u32[]{:S(2)}, u32[]{:S(2)}) async-start(bf16[128,3,3584]{2,1,0:T(4,128)(2,1)} %reshape.94), calls=%async_computation | async-start | bytes 7340032 | tf_op jit(solution)/shard_map/all_to_all | solution.py:95
  58.7 4.1 %reshape.100 = bf16[256,3584]{1,0:T(8,128)(2,1)S(1)} reshape(bf16[128,2,3584]{2,1,0:T(2,128)(2,1)} %all-to-all-done.2) | data formatting | bytes 3670016 | tf_op jit(solution)/shard_map/reshape | solution.py:96
  62.8 3.8 %fusion.8 = f32[256,1024]{1,0:T(8,128)S(1)} fusion(bf16[1,1792,1024]{2,1,0:T(8,128)(2,1)} %param.12, bf16[256,3584]{1,0:T(8,128)(2,1)S(1)} %reshape.100), kind=kOutput, calls=%fused_computation.14 | convolution fusion | flops 939524096 | bytes 5636096 | tf_op jit(solution)/shard_map/dot_general | solution.py:100
  66.7 1.1 fusion.2
  67.9 0.9 copy-done.8
  68.7 1.2 fusion.16
  70.3 1.7 copy-done
  71.9 1.4 convert_element_type.118
  73.3 32.6 %all-to-all-done = bf16[128,3,3584]{2,1,0:T(4,128)(2,1)} async-done(((bf16[128,3,3584]{2,1,0:T(4,128)(2,1)}), bf16[128,3,3584]{2,1,0:T(4,128)(2,1)}, u32[]{:S(2)}, u32[]{:S(2)}) %all-to-all-start) | async-done | bytes 2752544 | tf_op jit(solution)/shard_map/all_to_all | solution.py:95
  105.9 4.4 %all-to-all-start.3 = ((bf16[4,64,3072]{2,1,0:T(8,128)(2,1)}), bf16[4,64,3072]{2,1,0:T(8,128)(2,1)}, u32[]{:S(2)}, u32[]{:S(2)}) async-start(bf16[4,64,3072]{2,1,0:T(8,128)(2,1)} %convert_element_type.118), calls=%async_computation.3 | async-start | bytes 3145728 | tf_op jit(solution)/shard_map/all_to_all | solution.py:27
  110.5 5.6 %reshape.95 = bf16[384,3584]{1,0:T(8,128)(2,1)S(1)} reshape(bf16[128,3,3584]{2,1,0:T(4,128)(2,1)} %all-to-all-done) | data formatting | bytes 5505024 | tf_op jit(solution)/shard_map/reshape | solution.py:96
  116.2 5.0 %fusion.12 = f32[384,1024]{1,0:T(8,128)} fusion(bf16[1,1792,1024]{2,1,0:T(8,128)(2,1)} %param.12, bf16[384,3584]{1,0:T(8,128)(2,1)S(1)} %reshape.95), kind=kOutput, calls=%fused_computation.18 | convolution fusion | flops 1409286144 | bytes 6619136 | tf_op jit(solution)/shard_map/dot_general | solution.py:100
  121.2 2.8 fusion.4
  123.9 2.8 fusion.20
  126.7 3.3 %all-to-all-done.3 = bf16[4,64,3072]{2,1,0:T(8,128)(2,1)} async-done(((bf16[4,64,3072]{2,1,0:T(8,128)(2,1)}), bf16[4,64,3072]{2,1,0:T(8,128)(2,1)}, u32[]{:S(2)}, u32[]{:S(2)}) %all-to-all-start.3) | async-done | bytes 1572896 | tf_op jit(solution)/shard_map/all_to_all | solution.py:27
  130.1 1.9 multiply_reduce_fusion
  131.9 1.3 bitcast_add_fusion.1
  134.2 2.7 pad_maximum_fusion
  137.5 2.4 collective-permute-start.2
  139.9 18.6 %collective-permute-done = bf16[96,3072]{1,0:T(8,128)(2,1)S(1)} collective-permute-done((bf16[96,3072]{1,0:T(8,128)(2,1)S(1)}, bf16[96,3072]{1,0:T(8,128)(2,1)S(1)}, u32[]{:S(2)}, u32[]{:S(2)}) %collective-permute-start) | collective-permute-done | bytes 589856 | tf_op jit(solution)/shard_map/ppermute | solution.py:42
  158.5 4.1 %collective-permute-done.2 = bf16[96,3072]{1,0:T(8,128)(2,1)S(1)} collective-permute-done((bf16[96,3072]{1,0:T(8,128)(2,1)S(1)}, bf16[96,3072]{1,0:T(8,128)(2,1)S(1)}, u32[]{:S(2)}, u32[]{:S(2)}) %collective-permute-start.2) | collective-permute-done | bytes 589856 | tf_op jit(solution)/shard_map/ppermute | solution.py:42
  162.5 13.4 %collective-permute-done.1 = bf16[96,3072]{1,0:T(8,128)(2,1)S(1)} collective-permute-done((bf16[96,3072]{1,0:T(8,128)(2,1)S(1)}, bf16[96,3072]{1,0:T(8,128)(2,1)S(1)}, u32[]{:S(2)}, u32[]{:S(2)}) %collective-permute-start.1) | collective-permute-done | bytes 589856 | tf_op jit(solution)/shard_map/ppermute | solution.py:42
  176.5 0.9 pad_maximum_fusion.3
  177.4 1.8 all-gather.5.cloned.1.call-done
  179.2 3.5 %fusion.6 = f32[256,1792]{1,0:T(8,128)S(1)} fusion(bf16[1,1792,1024]{2,1,0:T(8,128)(2,1)} %param.12, bf16[256,3072]{1,0:T(8,128)(2,1)} %all-gather.5.cloned.1.call-done), kind=kOutput, calls=%fused_computation.12 | convolution fusion | flops 939524096 | bytes 6029312 | tf_op jit(solution)/shard_map/dot_general | solution.py:117
  182.7 3.1 %fusion.34 = bf16[256,1792]{1,0:T(8,128)(2,1)} fusion(f32[256,1792]{1,0:T(8,128)S(1)} %fusion.6, bf16[1,1792,1024]{2,1,0:T(8,128)(2,1)S(1)} %copy-done.10, bf16[256,3072]{1,0:T(8,128)(2,1)} %all-gather.5.cloned.1.call-done), kind=kOutput, calls=%fused_computation.36 | convolution fusion | flops 940441600 | bytes 6946816 | tf_op jit(solution)/shard_map/dot_general | solution.py:115
  185.9 3.1 %reshape.102 = bf16[128,2,1792]{2,1,0:T(2,128)(2,1)} reshape(bf16[256,1792]{1,0:T(8,128)(2,1)} %fusion.34) | data formatting | bytes 1835008 | tf_op jit(solution)/shard_map/reshape | solution.py:126
  188.9 34.5 %all_to_all.25 = bf16[128,2,1792]{2,1,0:T(2,128)(2,1)S(1)} all-to-all(bf16[128,2,1792]{2,1,0:T(2,128)(2,1)} %reshape.102), channel_id=1, replica_groups=mesh['expert'=32,'dp'=4] {'dp','expert'}, dimensions={0} | all-to-all | bytes 1835008 | tf_op jit(solution)/shard_map/all_to_all | solution.py:127
  223.4 1.7 copy.61
  225.1 4.1 %fusion.10 = f32[384,1792]{1,0:T(8,128)S(1)} fusion(bf16[1,1792,1024]{2,1,0:T(8,128)(2,1)} %param.12, bf16[384,3072]{1,0:T(8,128)(2,1)} %all-gather.3.cloned.1.call-done), kind=kOutput, calls=%fused_computation.16 | convolution fusion | flops 1409286144 | bytes 7208960 | tf_op jit(solution)/shard_map/dot_general | solution.py:117
  229.2 3.9 %fusion.28 = bf16[384,1792]{1,0:T(8,128)(2,1)} fusion(f32[384,1792]{1,0:T(8,128)S(1)} %fusion.10, bf16[1,1792,1024]{2,1,0:T(8,128)(2,1)S(1)} %copy-done.11, bf16[384,3072]{1,0:T(8,128)(2,1)} %all-gather.3.cloned.1.call-done), kind=kOutput, calls=%fused_computation.34 | convolution fusion | flops 1410662400 | bytes 8585216 | tf_op jit(solution)/shard_map/dot_general | solution.py:115
  233.1 3.8 %reshape.97 = bf16[128,3,1792]{2,1,0:T(4,128)(2,1)} reshape(bf16[384,1792]{1,0:T(8,128)(2,1)} %fusion.28) | data formatting | bytes 2752512 | tf_op jit(solution)/shard_map/reshape | solution.py:126
  236.9 5.8 %all-to-all-start.1 = ((bf16[128,3,1792]{2,1,0:T(4,128)(2,1)}), bf16[128,3,1792]{2,1,0:T(4,128)(2,1)}, u32[]{:S(2)}, u32[]{:S(2)}) async-start(bf16[128,3,1792]{2,1,0:T(4,128)(2,1)} %reshape.97), calls=%async_computation.1 | async-start | bytes 3670016 | tf_op jit(solution)/shard_map/all_to_all | solution.py:127
  242.7 3.4 %fusion.48 = f32[1792,1024]{1,0:T(8,128)S(1)} fusion(bf16[384,3584]{1,0:T(8,128)(2,1)S(1)} %reshape.95, bf16[384,3072]{1,0:T(8,128)(2,1)} %all-gather.3.cloned.1.call-done), kind=kOutput, calls=%fused_computation.52 | convolution fusion | flops 1409286144 | bytes 9502720 | tf_op jit(solution)/shard_map/dot_general | solution.py:17
  246.2 2.1 fusion.46
  248.3 3.0 %fusion.22 = bf16[1,1792,1024]{2,1,0:T(8,128)(2,1)} fusion(f32[1792,1024]{1,0:T(8,128)S(1)} %fusion.48, bf16[256,3584]{1,0:T(8,128)(2,1)S(1)} %copy-done.2, bf16[256,3072]{1,0:T(8,128)(2,1)S(1)} %copy-done.5), kind=kOutput, calls=%fused_computation.28 | convolution fusion | flops 943194112 | bytes 12451840 | tf_op jit(solution)/shard_map/dot_general | solution.py:17
  251.3 2.1 fusion.41
  253.4 3.0 %fusion.23 = bf16[1,1792,1024]{2,1,0:T(8,128)(2,1)} fusion(f32[1792,1024]{1,0:T(8,128)S(1)} %fusion.46, bf16[256,3584]{1,0:T(8,128)(2,1)S(1)} %copy-done.2, bf16[256,3072]{1,0:T(8,128)(2,1)S(1)} %copy-done.5), kind=kOutput, calls=%fused_computation.29 | convolution fusion | flops 943194112 | bytes 12451840 | tf_op jit(solution)/shard_map/dot_general | solution.py:17
  256.4 3.0 %fusion.24 = bf16[1,1024,1792]{2,1,0:T(8,128)(2,1)} fusion(f32[1024,1792]{1,0:T(8,128)S(1)} %fusion.41, bf16[256,3584]{1,0:T(8,128)(2,1)S(1)} %copy-done.2, bf16[256,3072]{1,0:T(8,128)(2,1)S(1)} %copy-done.5), kind=kOutput, calls=%fused_computation.30 | convolution fusion | flops 943194112 | bytes 12451840 | tf_op jit(solution)/shard_map/dot_general | solution.py:17
  259.5 10.5 %all-to-all-done.1 = bf16[128,3,1792]{2,1,0:T(4,128)(2,1)} async-done(((bf16[128,3,1792]{2,1,0:T(4,128)(2,1)}), bf16[128,3,1792]{2,1,0:T(4,128)(2,1)}, u32[]{:S(2)}, u32[]{:S(2)}) %all-to-all-start.1) | async-done | bytes 1376288 | tf_op jit(solution)/shard_map/all_to_all | solution.py:127
  270.0 2.8 copy.60
  272.8 1.5 pad_maximum_fusion.2
  (65 shorter events, 8.1 us)
Async XLA Ops:
  13.7 39.2 %all-to-all-start.2 = ((bf16[128,2,3584]{2,1,0:T(2,128)(2,1)}), bf16[128,2,3584]{2,1,0:T(2,128)(2,1)}, u32[]{:S(2)}, u32[]{:S(2)}) async-start(bf16[128,2,3584]{2,1,0:T(2,128)(2,1)} %reshape.99), calls=%async_computation.2 | async-start | bytes 3670016 | tf_op jit(solution)/shard_map/all_to_all | solution.py:95
  53.0 53.0 %all-to-all-start = ((bf16[128,3,3584]{2,1,0:T(4,128)(2,1)}), bf16[128,3,3584]{2,1,0:T(4,128)(2,1)}, u32[]{:S(2)}, u32[]{:S(2)}) async-start(bf16[128,3,3584]{2,1,0:T(4,128)(2,1)} %reshape.94), calls=%async_computation | async-start | bytes 7340032 | tf_op jit(solution)/shard_map/all_to_all | solution.py:95
  62.8 5.0 %copy-start.1 = (bf16[256,3584]{1,0:T(8,128)(2,1)}, bf16[256,3584]{1,0:T(8,128)(2,1)S(1)}, u32[]{:S(2)}) copy-start(bf16[256,3584]{1,0:T(8,128)(2,1)S(1)} %reshape.100) | copy-start | bytes 5505028
  62.8 3.9 %copy-start.6 = (bf16[1,1024,1792]{2,1,0:T(8,128)(2,1)S(1)}, bf16[1,1024,1792]{2,1,0:T(8,128)(2,1)}, u32[]{:S(2)}) copy-start(bf16[1,1024,1792]{2,1,0:T(8,128)(2,1)} %param.13) | copy-start | bytes 11010052
  66.7 2.0 copy-start.8
  70.3 1.7 copy-start
  105.9 24.1 %all-to-all-start.3 = ((bf16[4,64,3072]{2,1,0:T(8,128)(2,1)}), bf16[4,64,3072]{2,1,0:T(8,128)(2,1)}, u32[]{:S(2)}, u32[]{:S(2)}) async-start(bf16[4,64,3072]{2,1,0:T(8,128)(2,1)} %convert_element_type.118), calls=%async_computation.3 | async-start | bytes 3145728 | tf_op jit(solution)/shard_map/all_to_all | solution.py:27
  110.3 68.9 %all-gather.5.cloned.1.call-start = ((), (), s32[]{:S(2)}) async-start(), calls=%async_computation.6 | async-start | bytes 1966080 | tf_op jit(solution)/shard_map/all_gather | solution.py:109
  116.2 5.0 %copy-start.7 = (bf16[1,1024,1792]{2,1,0:T(8,128)(2,1)S(1)}, bf16[1,1024,1792]{2,1,0:T(8,128)(2,1)}, u32[]{:S(2)}) copy-start(bf16[1,1024,1792]{2,1,0:T(8,128)(2,1)} %param.13) | copy-start | bytes 11010052
  121.1 2.8 copy-start.9
  134.1 91.0 %all-gather.3.cloned.1.call-start = ((), (), s32[]{:S(2)}) async-start(), calls=%async_computation.5 | async-start | bytes 2949120 | tf_op jit(solution)/shard_map/all_gather | solution.py:109
  137.1 21.3 %collective-permute-start = (bf16[96,3072]{1,0:T(8,128)(2,1)S(1)}, bf16[96,3072]{1,0:T(8,128)(2,1)S(1)}, u32[]{:S(2)}, u32[]{:S(2)}) collective-permute-start(bf16[96,3072]{1,0:T(8,128)(2,1)S(1)} %get-tuple-element.4), channel_id=1, source_target_pairs={{0,1},{1,2},{2,3},{3,0},{4,5},{5,6},{6,7},{7,4},{8,9},{9,10},{10,1... | collective-permute-start | bytes 1769480 | tf_op jit(solution)/shard_map/ppermute | solution.py:42
  137.5 25.1 %collective-permute-start.2 = (bf16[96,3072]{1,0:T(8,128)(2,1)S(1)}, bf16[96,3072]{1,0:T(8,128)(2,1)S(1)}, u32[]{:S(2)}, u32[]{:S(2)}) collective-permute-start(bf16[96,3072]{1,0:T(8,128)(2,1)S(1)} %get-tuple-element.5), channel_id=1, source_target_pairs={{0,3},{1,0},{2,1},{3,2},{4,7},{5,4},{6,5},{7,6},{8,11},{9,8},{10,9... | collective-permute-start | bytes 1769480 | tf_op jit(solution)/shard_map/ppermute | solution.py:42
  139.9 36.1 %collective-permute-start.1 = (bf16[96,3072]{1,0:T(8,128)(2,1)S(1)}, bf16[96,3072]{1,0:T(8,128)(2,1)S(1)}, u32[]{:S(2)}, u32[]{:S(2)}) collective-permute-start(bf16[96,3072]{1,0:T(8,128)(2,1)S(1)} %get-tuple-element.6), channel_id=1, source_target_pairs={{0,2},{1,3},{2,0},{3,1},{4,6},{5,7},{6,4},{7,5},{8,10},{9,11},{10,... | collective-permute-start | bytes 1769480 | tf_op jit(solution)/shard_map/ppermute | solution.py:42
  179.2 3.5 %copy-start.10 = (bf16[1,1792,1024]{2,1,0:T(8,128)(2,1)S(1)}, bf16[1,1792,1024]{2,1,0:T(8,128)(2,1)}, u32[]{:S(2)}) copy-start(bf16[1,1792,1024]{2,1,0:T(8,128)(2,1)} %param.11) | copy-start | bytes 11010052
  225.1 4.1 %copy-start.11 = (bf16[1,1792,1024]{2,1,0:T(8,128)(2,1)S(1)}, bf16[1,1792,1024]{2,1,0:T(8,128)(2,1)}, u32[]{:S(2)}) copy-start(bf16[1,1792,1024]{2,1,0:T(8,128)(2,1)} %param.11) | copy-start | bytes 11010052
  236.9 33.0 %all-to-all-start.1 = ((bf16[128,3,1792]{2,1,0:T(4,128)(2,1)}), bf16[128,3,1792]{2,1,0:T(4,128)(2,1)}, u32[]{:S(2)}, u32[]{:S(2)}) async-start(bf16[128,3,1792]{2,1,0:T(4,128)(2,1)} %reshape.97), calls=%async_computation.1 | async-start | bytes 3670016 | tf_op jit(solution)/shard_map/all_to_all | solution.py:127
  242.7 3.4 %copy-start.4 = (bf16[384,3072]{1,0:T(8,128)(2,1)S(1)}, bf16[384,3072]{1,0:T(8,128)(2,1)}, u32[]{:S(2)}) copy-start(bf16[384,3072]{1,0:T(8,128)(2,1)} %all-gather.3.cloned.1.call-done) | copy-start | bytes 7077892
  246.1 2.1 copy-start.2
  246.2 2.1 copy-start.5
  259.4 13.3 %copy-start.3 = (bf16[4,32,2,1792]{3,0,2,1:T(4,128)(2,1)S(1)}, bf16[4,32,2,1792]{3,0,2,1:T(4,128)(2,1)}, u32[]{:S(2)}) copy-start(bf16[4,32,2,1792]{3,0,2,1:T(4,128)(2,1)} %copy.61) | copy-start | bytes 2752516
Sparse Core Ops, SparseCore 0:
  134.3 44.9 all-gather.4
  180.9 40.6 all-gather.2

commit v5 on v2

--- a/solution.py
+++ b/solution.py
@@ -62,7 +62,7 @@
     axes = ("dp", "expert")
     split = (capacity + 1) // 2
     bounds = [(0, split), (split, capacity)]
-    sums = [None, None, None]
+    kept = []
     pieces = []
     for lo, hi in bounds:
         take = hi - lo
@@ -104,16 +104,16 @@
         ) + lax.dot_general(
             grad_lin, up_local, (((1,), (1,)), ((), ())), preferred_element_type=jnp.float32
         )
-        terms = (
-            contract_rows(act_rows, grad_pre),
-            contract_rows(act_rows, grad_lin),
-            contract_rows(activated, cot_rows),
-        )
-        sums = [t if s is None else s + t for s, t in zip(sums, terms)]
+        kept.append((act_rows, cot_rows, grad_pre, grad_lin, activated))
         flat_back = rows_back.astype(jnp.bfloat16).reshape(num_dp * num_exp, take, slice_width)
         arrived = lax.all_to_all(flat_back, axes, split_axis=0, concat_axis=0, tiled=True)
         pieces.append(arrived.reshape(num_dp, num_exp, take, slice_width))
-    grad_gate, grad_up, grad_down = (s.astype(jnp.bfloat16)[None] for s in sums)
+    act_all, cot_all, pre_all, lin_all, activated_all = (
+        jnp.concatenate(group, axis=0) for group in zip(*kept)
+    )
+    grad_gate = contract_rows(act_all, pre_all).astype(jnp.bfloat16)[None]
+    grad_up = contract_rows(act_all, lin_all).astype(jnp.bfloat16)[None]
+    grad_down = contract_rows(activated_all, cot_all).astype(jnp.bfloat16)[None]
     arrived = jnp.concatenate(pieces, axis=2).reshape(num_dp, num_exp * capacity, slice_width)
     spread = jnp.broadcast_to(placing[None], (num_dp,) + placing.shape)
     grad_slices = lax.dot_general(

time: 279 us -> 271 us (0.971)
  blocking collectives: 36.2 us -> 0 us
  waiting for transfers between devices: 109 us -> 130 us
  starting transfers between devices: 30.7 us -> 41.8 us
  matrix products: 46.4 us -> 41.3 us
    all_to_all x1 -> x0, blocking collectives: 36.2 us -> none  [shards(): lax.all_to_all(flat_back, axes, split_axis=0, concat_axis=0, tiled=True)]
    all_gather x2, waiting for transfers between devices: 0.02 us -> 22.7 us  [shards(): lax.all_gather(jnp.concatenate([grad_pre, grad_lin, activated], axis=1),...]
    all_to_all x1 -> x2, starting transfers between devices: 5.79 us -> 16.9 us  [shards(): lax.all_to_all(flat_back, axes, split_axis=0, concat_axis=0, tiled=True)]
    slice x0 -> x4, local copies, waits for them, and re-layouts: none -> 6.37 us  [the longest x2 4.51 us: shards(): cot_rows = recv_both[:, slice_width:]]
    reshape x2, local copies, waits for them, and re-layouts: 6.9 us -> 3.33 us  [shards(): rows_back.astype(jnp.bfloat16).reshape(num_dp * num_exp, take, slice_width)]
    dot_general x6 -> x3, matrix products: 16.6 us -> 13.6 us  [contract_rows(): lax.dot_general(left, right, (((0,), (0,)), ((), ())), preferred_element_...]
    all_to_all x1 -> x2, waiting for transfers between devices: 10.5 us -> 9.12 us  [shards(): lax.all_to_all(flat_back, axes, split_axis=0, concat_axis=0, tiled=True)]
  transfers between devices with their start and end apart: 11 -> 12, of which waited for: 6 -> 7; matrix products, arithmetic and copies ran while one was open for 22% -> 26% of each run, Pallas kernels for 0% -> 0%
where the time goes in v5:
time: 271 us
  waiting for transfers between devices  130 us (48%)
  starting transfers between devices  41.8 us (15%)
  matrix products  41.3 us (15%)
  local copies, waits for them, and re-layouts  35.9 us (13%)
  between operations  14.6 us (5%)
  other arithmetic  6.6 us (2%)
    ppermute x6, waiting for transfers between devices, exchange(): came = lax.ppermute(block.astype(jnp.bfloat16), 'dp', pairs)  76.7 us
    all_gather x2, waiting for transfers between devices, shards(): lax.all_gather(jnp.concatenate([grad_pre, grad_lin, activated], axis=1),...  22.7 us
    all_to_all x2, waiting for transfers between devices, shards(): lax.all_to_all(flat_both, axes, split_axis=0, concat_axis=0, tiled=True)  21.8 us
    all_to_all x2, starting transfers between devices, shards(): lax.all_to_all(flat_both, axes, split_axis=0, concat_axis=0, tiled=True)  17.6 us
    all_to_all x2, starting transfers between devices, shards(): lax.all_to_all(flat_back, axes, split_axis=0, concat_axis=0, tiled=True)  16.9 us
    dot_general x3, matrix products, contract_rows(): lax.dot_general(left, right, (((0,), (0,)), ((), ())), preferred_element_...  13.6 us
    reshape x2, local copies, waits for them, and re-layouts, shards(): recv_both = recv_both.reshape(num_exp * num_dp * take, 2 * slice_width)  9.71 us
    all_to_all x2, waiting for transfers between devices, shards(): lax.all_to_all(flat_back, axes, split_axis=0, concat_axis=0, tiled=True)  9.12 us
  transfers between devices with their start and end apart: 12, of which 7 were waited for; matrix products, arithmetic and copies ran while one was open for 26% of the time, Pallas kernels for 0%

profile of v5, /device:TPU:1, one launch (start us, length us, event | category | flops | bytes accessed | tf_op | source)
XLA Modules:
  0.0 270.5 jit_solution(9096746041630390274)
XLA Ops:
  7.2 0.8 copy.51
  11.1 1.6 reshape.97
  12.8 11.9 %all-to-all-start.2 = ((bf16[128,2,3584]{2,1,0:T(2,128)(2,1)}), bf16[128,2,3584]{2,1,0:T(2,128)(2,1)}, u32[]{:S(2)}, u32[]{:S(2)}) async-start(bf16[128,2,3584]{2,1,0:T(2,128)(2,1)} %reshape.97), calls=%async_computation.2 | async-start | bytes 3670016 | tf_op jit(solution)/shard_map/all_to_all | solution.py:83
  25.2 0.9 fusion
  26.1 4.0 %reshape.92 = bf16[128,3,3584]{2,1,0:T(4,128)(2,1)} reshape(bf16[4,96,3584]{2,1,0:T(8,128)(2,1)S(1)} %fusion) | data formatting | bytes 5505024 | tf_op jit(solution)/shard_map/reshape | solution.py:82
  30.2 21.8 %all-to-all-done.2 = bf16[128,2,3584]{2,1,0:T(2,128)(2,1)} async-done(((bf16[128,2,3584]{2,1,0:T(2,128)(2,1)}), bf16[128,2,3584]{2,1,0:T(2,128)(2,1)}, u32[]{:S(2)}, u32[]{:S(2)}) %all-to-all-start.2) | async-done | bytes 1835040 | tf_op jit(solution)/shard_map/all_to_all | solution.py:83
  52.0 5.7 %all-to-all-start = ((bf16[128,3,3584]{2,1,0:T(4,128)(2,1)}), bf16[128,3,3584]{2,1,0:T(4,128)(2,1)}, u32[]{:S(2)}, u32[]{:S(2)}) async-start(bf16[128,3,3584]{2,1,0:T(4,128)(2,1)} %reshape.92), calls=%async_computation | async-start | bytes 7340032 | tf_op jit(solution)/shard_map/all_to_all | solution.py:83
  57.8 4.1 %reshape.98 = bf16[256,3584]{1,0:T(8,128)(2,1)S(1)} reshape(bf16[128,2,3584]{2,1,0:T(2,128)(2,1)} %all-to-all-done.2) | data formatting | bytes 3670016 | tf_op jit(solution)/shard_map/reshape | solution.py:84
  61.9 3.8 %fusion.8 = f32[256,1024]{1,0:T(8,128)S(1)} fusion(bf16[1,1792,1024]{2,1,0:T(8,128)(2,1)} %param.12, bf16[256,3584]{1,0:T(8,128)(2,1)S(1)} %reshape.98), kind=kOutput, calls=%fused_computation.14 | convolution fusion | flops 939524096 | bytes 5636096 | tf_op jit(solution)/shard_map/dot_general | solution.py:88
  65.7 1.1 fusion.2
  66.9 0.9 copy-done.11
  67.8 1.1 fusion.16
  69.1 1.0 fusion.60
  70.1 1.4 collective-permute-start.3
  71.5 1.3 collective-permute-start.5
  72.8 1.7 collective-permute-start.4
  74.5 33.5 %collective-permute-done.3 = bf16[64,3072]{1,0:T(8,128)(2,1)} collective-permute-done((bf16[64,3072]{1,0:T(8,128)(2,1)}, bf16[64,3072]{1,0:T(8,128)(2,1)}, u32[]{:S(2)}, u32[]{:S(2)}) %collective-permute-start.3) | collective-permute-done | bytes 393248 | tf_op jit(solution)/shard_map/ppermute | solution.py:30
  108.0 8.5 %collective-permute-done.4 = bf16[64,3072]{1,0:T(8,128)(2,1)} collective-permute-done((bf16[64,3072]{1,0:T(8,128)(2,1)S(1)}, bf16[64,3072]{1,0:T(8,128)(2,1)}, u32[]{:S(2)}, u32[]{:S(2)}) %collective-permute-start.4) | collective-permute-done | bytes 393248 | tf_op jit(solution)/shard_map/ppermute | solution.py:30
  116.5 1.4 fusion.56
  118.0 0.8 pad_maximum_fusion.8
  119.1 5.6 %reshape.93 = bf16[384,3584]{1,0:T(8,128)(2,1)S(1)} reshape(bf16[128,3,3584]{2,1,0:T(4,128)(2,1)} %all-to-all-done) | data formatting | bytes 5505024 | tf_op jit(solution)/shard_map/reshape | solution.py:84
  124.7 3.8 %fusion.12 = f32[384,1024]{1,0:T(8,128)S(1)} fusion(bf16[1,1792,1024]{2,1,0:T(8,128)(2,1)} %param.12, bf16[384,3584]{1,0:T(8,128)(2,1)S(1)} %reshape.93), kind=kOutput, calls=%fused_computation.18 | convolution fusion | flops 1409286144 | bytes 6619136 | tf_op jit(solution)/shard_map/dot_general | solution.py:88
  128.5 1.6 fusion.4
  130.8 1.7 fusion.20
  133.6 2.4 collective-permute-start.2
  136.0 21.8 %collective-permute-done = bf16[96,3072]{1,0:T(8,128)(2,1)S(1)} collective-permute-done((bf16[96,3072]{1,0:T(8,128)(2,1)S(1)}, bf16[96,3072]{1,0:T(8,128)(2,1)S(1)}, u32[]{:S(2)}, u32[]{:S(2)}) %collective-permute-start) | collective-permute-done | bytes 589856 | tf_op jit(solution)/shard_map/ppermute | solution.py:30
  157.7 12.9 %collective-permute-done.1 = bf16[96,3072]{1,0:T(8,128)(2,1)S(1)} collective-permute-done((bf16[96,3072]{1,0:T(8,128)(2,1)S(1)}, bf16[96,3072]{1,0:T(8,128)(2,1)S(1)}, u32[]{:S(2)}, u32[]{:S(2)}) %collective-permute-start.1) | collective-permute-done | bytes 589856 | tf_op jit(solution)/shard_map/ppermute | solution.py:30
  171.2 0.9 pad_maximum_fusion.6
  172.1 2.8 %fusion.87 = (bf16[256,1792]{1,0:T(8,128)(2,1)}, bf16[256,1792]{1,0:T(8,128)(2,1)}) fusion(bf16[256,3584]{1,0:T(8,128)(2,1)} %copy-done), kind=kLoop, calls=%fused_computation.114 | loop fusion | bytes 3670016 | tf_op jit(solution)/shard_map/slice | solution.py:86
  174.9 1.7 fusion.85
  176.6 3.5 %fusion.6 = f32[256,1792]{1,0:T(8,128)S(1)} fusion(bf16[1,1792,1024]{2,1,0:T(8,128)(2,1)} %param.12, bf16[256,3072]{1,0:T(8,128)(2,1)} %all-gather.5.cloned.1.call-done), kind=kOutput, calls=%fused_computation.12 | convolution fusion | flops 939524096 | bytes 6029312 | tf_op jit(solution)/shard_map/dot_general | solution.py:104
  180.1 2.2 fusion.34
  182.3 1.3 reshape.100
  183.6 8.1 %all-to-all-start.3 = ((bf16[128,2,1792]{2,1,0:T(2,128)(2,1)}), bf16[128,2,1792]{2,1,0:T(2,128)(2,1)S(1)}, u32[]{:S(2)}, u32[]{:S(2)}) async-start(bf16[128,2,1792]{2,1,0:T(2,128)(2,1)} %reshape.100), calls=%async_computation.3 | async-start | bytes 1835008 | tf_op jit(solution)/shard_map/all_to_all | solution.py:109
  191.7 22.7 %all-gather.3.cloned.1.call-done = bf16[384,3072]{1,0:T(8,128)(2,1)} async-done(((bf16[96,3072]{1,0:T(8,128)(2,1)}), bf16[384,3072]{1,0:T(8,128)(2,1)}) %all-gather.3.cloned.1.call-update) | async-done | bytes 2359312 | tf_op jit(solution)/shard_map/all_gather | solution.py:96
  214.4 4.1 %fusion.10 = f32[384,1792]{1,0:T(8,128)S(1)} fusion(bf16[1,1792,1024]{2,1,0:T(8,128)(2,1)} %param.12, bf16[384,3072]{1,0:T(8,128)(2,1)} %all-gather.3.cloned.1.call-done), kind=kOutput, calls=%fused_computation.16 | convolution fusion | flops 1409286144 | bytes 7208960 | tf_op jit(solution)/shard_map/dot_general | solution.py:104
  218.4 2.8 %fusion.28 = bf16[384,1792]{1,0:T(8,128)(2,1)S(1)} fusion(f32[384,1792]{1,0:T(8,128)S(1)} %fusion.10, bf16[1,1792,1024]{2,1,0:T(8,128)(2,1)S(1)} %copy-done.14, bf16[384,3072]{1,0:T(8,128)(2,1)} %all-gather.3.cloned.1.call-done), kind=kOutput, calls=%fused_computation.33 | convolution fusion | flops 1410662400 | bytes 8585216 | tf_op jit(solution)/shard_map/dot_general | solution.py:102
  221.3 2.1 reshape.95
  223.3 8.8 %all-to-all-start.1 = ((bf16[128,3,1792]{2,1,0:T(4,128)(2,1)}), bf16[128,3,1792]{2,1,0:T(4,128)(2,1)S(1)}, u32[]{:S(2)}, u32[]{:S(2)}) async-start(bf16[128,3,1792]{2,1,0:T(4,128)(2,1)} %reshape.95), calls=%async_computation.1 | async-start | bytes 3670016 | tf_op jit(solution)/shard_map/all_to_all | solution.py:109
  232.1 1.6 fusion.88
  233.8 1.7 copy.61
  235.7 1.1 copy-done.4
  237.0 4.5 %fusion.23 = bf16[1,1792,1024]{2,1,0:T(8,128)(2,1)} fusion(bf16[256,1792]{1,0:T(8,128)(2,1)S(1)} %copy-done.6, bf16[384,1792]{1,0:T(8,128)(2,1)S(1)} %copy-done.4, bf16[256,1024]{1,0:T(8,128)(2,1)S(1)} %get-tuple-element.18, bf16[384,1024]{1,0:T(8,128)(2,1)S(1)} %get-tuple-element.13), kind=kOutput, calls=%fused_computation.29 | convolution fusion | flops 2357854208 | bytes 7274496 | tf_op jit(solution)/shard_map/dot_general | solution.py:17
  241.6 4.5 %fusion.22 = bf16[1,1792,1024]{2,1,0:T(8,128)(2,1)} fusion(bf16[256,1792]{1,0:T(8,128)(2,1)S(1)} %copy-done.6, bf16[384,1792]{1,0:T(8,128)(2,1)S(1)} %copy-done.4, bf16[256,1024]{1,0:T(8,128)(2,1)S(1)} %get-tuple-element.19, bf16[384,1024]{1,0:T(8,128)(2,1)S(1)} %get-tuple-element.14), kind=kOutput, calls=%fused_computation.28 | convolution fusion | flops 2357854208 | bytes 7274496 | tf_op jit(solution)/shard_map/dot_general | solution.py:17
  246.1 4.5 %fusion.24 = bf16[1,1024,1792]{2,1,0:T(8,128)(2,1)} fusion(bf16[256,1792]{1,0:T(8,128)(2,1)S(1)} %copy-done.5, bf16[384,1792]{1,0:T(8,128)(2,1)S(1)} %copy-done.3, bf16[256,1024]{1,0:T(8,128)(2,1)S(1)} %get-tuple-element.17, bf16[384,1024]{1,0:T(8,128)(2,1)S(1)} %get-tuple-element.12), kind=kOutput, calls=%fused_computation.30 | convolution fusion | flops 2357854208 | bytes 7274496 | tf_op jit(solution)/shard_map/dot_general | solution.py:17
  250.6 9.1 %all-to-all-done.1 = bf16[128,3,1792]{2,1,0:T(4,128)(2,1)S(1)} async-done(((bf16[128,3,1792]{2,1,0:T(4,128)(2,1)}), bf16[128,3,1792]{2,1,0:T(4,128)(2,1)S(1)}, u32[]{:S(2)}, u32[]{:S(2)}) %all-to-all-start.1) | async-done | bytes 1376288 | tf_op jit(solution)/shard_map/all_to_all | solution.py:109
  259.7 1.3 copy.60
  261.1 1.5 pad_maximum_fusion.2
  (75 shorter events, 8.1 us)
Async XLA Ops:
  7.2 3.2 %copy-start.7 = (bf16[16,7168]{1,0:T(8,128)(2,1)S(1)}, bf16[16,7168]{1,0:T(8,128)(2,1)}, u32[]{:S(2)}) copy-start(bf16[16,7168]{1,0:T(8,128)(2,1)} %param.8) | copy-start | bytes 688132
  7.2 3.2 %copy-start.8 = (bf16[16,7168]{1,0:T(8,128)(2,1)S(1)}, bf16[16,7168]{1,0:T(8,128)(2,1)}, u32[]{:S(2)}) copy-start(bf16[16,7168]{1,0:T(8,128)(2,1)} %param.7) | copy-start | bytes 688132
  12.8 39.2 %all-to-all-start.2 = ((bf16[128,2,3584]{2,1,0:T(2,128)(2,1)}), bf16[128,2,3584]{2,1,0:T(2,128)(2,1)}, u32[]{:S(2)}, u32[]{:S(2)}) async-start(bf16[128,2,3584]{2,1,0:T(2,128)(2,1)} %reshape.97), calls=%async_computation.2 | async-start | bytes 3670016 | tf_op jit(solution)/shard_map/all_to_all | solution.py:83
  52.0 67.1 %all-to-all-start = ((bf16[128,3,3584]{2,1,0:T(4,128)(2,1)}), bf16[128,3,3584]{2,1,0:T(4,128)(2,1)}, u32[]{:S(2)}, u32[]{:S(2)}) async-start(bf16[128,3,3584]{2,1,0:T(4,128)(2,1)} %reshape.92), calls=%async_computation | async-start | bytes 7340032 | tf_op jit(solution)/shard_map/all_to_all | solution.py:83
  57.7 118.8 %all-gather.5.cloned.1.call-start = ((), (), s32[]{:S(2)}) async-start(), calls=%async_computation.5 | async-start | bytes 1966080 | tf_op jit(solution)/shard_map/all_gather | solution.py:96
  61.8 5.0 %copy-start = (bf16[256,3584]{1,0:T(8,128)(2,1)}, bf16[256,3584]{1,0:T(8,128)(2,1)S(1)}, u32[]{:S(2)}) copy-start(bf16[256,3584]{1,0:T(8,128)(2,1)S(1)} %reshape.98) | copy-start | bytes 5505028
  61.9 3.9 %copy-start.9 = (bf16[1,1024,1792]{2,1,0:T(8,128)(2,1)S(1)}, bf16[1,1024,1792]{2,1,0:T(8,128)(2,1)}, u32[]{:S(2)}) copy-start(bf16[1,1024,1792]{2,1,0:T(8,128)(2,1)} %param.13) | copy-start | bytes 11010052
  65.7 2.0 copy-start.11
  70.1 37.8 %collective-permute-start.3 = (bf16[64,3072]{1,0:T(8,128)(2,1)}, bf16[64,3072]{1,0:T(8,128)(2,1)}, u32[]{:S(2)}, u32[]{:S(2)}) collective-permute-start(bf16[64,3072]{1,0:T(8,128)(2,1)} %get-tuple-element.7), channel_id=1, source_target_pairs={{0,1},{1,2},{2,3},{3,0},{4,5},{5,6},{6,7},{7,4},{8,9},{9,10},{10,1... | collective-permute-start | bytes 1179656 | tf_op jit(solution)/shard_map/ppermute | solution.py:30
  71.5 36.5 %collective-permute-start.5 = (bf16[64,3072]{1,0:T(8,128)(2,1)}, bf16[64,3072]{1,0:T(8,128)(2,1)}, u32[]{:S(2)}, u32[]{:S(2)}) collective-permute-start(bf16[64,3072]{1,0:T(8,128)(2,1)} %get-tuple-element.8), channel_id=1, source_target_pairs={{0,3},{1,0},{2,1},{3,2},{4,7},{5,4},{6,5},{7,6},{8,11},{9,8},{10,9... | collective-permute-start | bytes 1179656 | tf_op jit(solution)/shard_map/ppermute | solution.py:30
  72.8 43.7 %collective-permute-start.4 = (bf16[64,3072]{1,0:T(8,128)(2,1)S(1)}, bf16[64,3072]{1,0:T(8,128)(2,1)}, u32[]{:S(2)}, u32[]{:S(2)}) collective-permute-start(bf16[64,3072]{1,0:T(8,128)(2,1)S(1)} %get-tuple-element.9), channel_id=1, source_target_pairs={{0,2},{1,3},{2,0},{3,1},{4,6},{5,7},{6,4},{7,5},{8,10},{9,11},{10,... | collective-permute-start | bytes 1179656 | tf_op jit(solution)/shard_map/ppermute | solution.py:30
  118.8 95.5 %all-gather.3.cloned.1.call-start = ((), (), s32[]{:S(2)}) async-start(), calls=%async_computation.4 | async-start | bytes 2949120 | tf_op jit(solution)/shard_map/all_gather | solution.py:96
  124.7 3.8 %copy-start.10 = (bf16[1,1024,1792]{2,1,0:T(8,128)(2,1)S(1)}, bf16[1,1024,1792]{2,1,0:T(8,128)(2,1)}, u32[]{:S(2)}) copy-start(bf16[1,1024,1792]{2,1,0:T(8,128)(2,1)} %param.13) | copy-start | bytes 11010052
  128.5 2.2 copy-start.12
  133.2 24.5 %collective-permute-start = (bf16[96,3072]{1,0:T(8,128)(2,1)S(1)}, bf16[96,3072]{1,0:T(8,128)(2,1)S(1)}, u32[]{:S(2)}, u32[]{:S(2)}) collective-permute-start(bf16[96,3072]{1,0:T(8,128)(2,1)S(1)} %get-tuple-element.4), channel_id=1, source_target_pairs={{0,1},{1,2},{2,3},{3,0},{4,5},{5,6},{6,7},{7,4},{8,9},{9,10},{10,1... | collective-permute-start | bytes 1769480 | tf_op jit(solution)/shard_map/ppermute | solution.py:30
  133.6 24.1 %collective-permute-start.2 = (bf16[96,3072]{1,0:T(8,128)(2,1)S(1)}, bf16[96,3072]{1,0:T(8,128)(2,1)S(1)}, u32[]{:S(2)}, u32[]{:S(2)}) collective-permute-start(bf16[96,3072]{1,0:T(8,128)(2,1)S(1)} %get-tuple-element.5), channel_id=1, source_target_pairs={{0,3},{1,0},{2,1},{3,2},{4,7},{5,4},{6,5},{7,6},{8,11},{9,8},{10,9... | collective-permute-start | bytes 1769480 | tf_op jit(solution)/shard_map/ppermute | solution.py:30
  136.0 34.7 %collective-permute-start.1 = (bf16[96,3072]{1,0:T(8,128)(2,1)S(1)}, bf16[96,3072]{1,0:T(8,128)(2,1)S(1)}, u32[]{:S(2)}, u32[]{:S(2)}) collective-permute-start(bf16[96,3072]{1,0:T(8,128)(2,1)S(1)} %get-tuple-element.6), channel_id=1, source_target_pairs={{0,2},{1,3},{2,0},{3,1},{4,6},{5,7},{6,4},{7,5},{8,10},{9,11},{10,... | collective-permute-start | bytes 1769480 | tf_op jit(solution)/shard_map/ppermute | solution.py:30
  176.6 3.5 %copy-start.13 = (bf16[1,1792,1024]{2,1,0:T(8,128)(2,1)S(1)}, bf16[1,1792,1024]{2,1,0:T(8,128)(2,1)}, u32[]{:S(2)}) copy-start(bf16[1,1792,1024]{2,1,0:T(8,128)(2,1)} %param.11) | copy-start | bytes 11010052
  183.6 39.7 %all-to-all-start.3 = ((bf16[128,2,1792]{2,1,0:T(2,128)(2,1)}), bf16[128,2,1792]{2,1,0:T(2,128)(2,1)S(1)}, u32[]{:S(2)}, u32[]{:S(2)}) async-start(bf16[128,2,1792]{2,1,0:T(2,128)(2,1)} %reshape.100), calls=%async_computation.3 | async-start | bytes 1835008 | tf_op jit(solution)/shard_map/all_to_all | solution.py:109
  214.4 4.1 %copy-start.14 = (bf16[1,1792,1024]{2,1,0:T(8,128)(2,1)S(1)}, bf16[1,1792,1024]{2,1,0:T(8,128)(2,1)}, u32[]{:S(2)}) copy-start(bf16[1,1792,1024]{2,1,0:T(8,128)(2,1)} %param.11) | copy-start | bytes 11010052
  223.3 36.4 %all-to-all-start.1 = ((bf16[128,3,1792]{2,1,0:T(4,128)(2,1)}), bf16[128,3,1792]{2,1,0:T(4,128)(2,1)S(1)}, u32[]{:S(2)}, u32[]{:S(2)}) async-start(bf16[128,3,1792]{2,1,0:T(4,128)(2,1)} %reshape.95), calls=%async_computation.1 | async-start | bytes 3670016 | tf_op jit(solution)/shard_map/all_to_all | solution.py:109
  232.1 3.3 %copy-start.2 = (bf16[384,3072]{1,0:T(8,128)(2,1)S(1)}, bf16[384,3072]{1,0:T(8,128)(2,1)}, u32[]{:S(2)}) copy-start(bf16[384,3072]{1,0:T(8,128)(2,1)} %all-gather.3.cloned.1.call-done) | copy-start | bytes 7077892
  235.4 1.3 copy-start.4
  235.4 1.6 copy-start.6
  241.6 4.5 %copy-start.3 = (bf16[384,1792]{1,0:T(8,128)(2,1)S(1)}, bf16[384,1792]{1,0:T(8,128)(2,1)}, u32[]{:S(2)}) copy-start(bf16[384,1792]{1,0:T(8,128)(2,1)} %get-tuple-element.10) | copy-start | bytes 4128772
  241.6 4.5 %copy-start.5 = (bf16[256,1792]{1,0:T(8,128)(2,1)S(1)}, bf16[256,1792]{1,0:T(8,128)(2,1)}, u32[]{:S(2)}) copy-start(bf16[256,1792]{1,0:T(8,128)(2,1)} %get-tuple-element.15) | copy-start | bytes 2752516
  250.6 10.4 %copy-start.1 = (bf16[4,32,2,1792]{3,0,2,1:T(4,128)(2,1)S(1)}, bf16[4,32,2,1792]{3,0,2,1:T(4,128)(2,1)}, u32[]{:S(2)}) copy-start(bf16[4,32,2,1792]{3,0,2,1:T(4,128)(2,1)} %copy.61) | copy-start | bytes 2752516
Sparse Core Ops, SparseCore 0:
  119.0 33.8 all-gather.4
  172.2 42.1 all-gather.2

commit v6 on v5

--- a/solution.py
+++ b/solution.py
@@ -64,21 +64,29 @@
     bounds = [(0, split), (split, capacity)]
     kept = []
     pieces = []
+    order = jnp.concatenate(
+        [slots[:, lo:hi].reshape(num_exp * (hi - lo), tok_rows) for lo, hi in bounds], axis=0
+    )
+    order_scale = jnp.concatenate(
+        [scale[:, lo:hi].reshape(num_exp * (hi - lo), 1) for lo, hi in bounds], axis=0
+    )
+    all_slots = num_exp * capacity
+    pick = jnp.broadcast_to(order[None], (num_dp, all_slots, tok_rows))
+    gathered_rows = lax.dot_general(
+        pick, both, (((2,), (1,)), ((0,), (0,))), preferred_element_type=jnp.float32
+    )
+    weight = jnp.concatenate(
+        [
+            jnp.ones((all_slots, slice_width), jnp.float32),
+            jnp.broadcast_to(order_scale, (all_slots, slice_width)),
+        ],
+        axis=1,
+    )
+    send_all = (gathered_rows * weight[None]).astype(jnp.bfloat16)
     for lo, hi in bounds:
         take = hi - lo
-        rows = num_exp * take
-        pick = jnp.broadcast_to(slots[:, lo:hi].reshape(1, rows, tok_rows), (num_dp, rows, tok_rows))
-        gathered_rows = lax.dot_general(
-            pick, both, (((2,), (1,)), ((0,), (0,))), preferred_element_type=jnp.float32
-        )
-        weight = jnp.concatenate(
-            [
-                jnp.ones((rows, slice_width), jnp.float32),
-                jnp.broadcast_to(scale[:, lo:hi].reshape(rows, 1), (rows, slice_width)),
-            ],
-            axis=1,
-        )
-        flat_both = (gathered_rows * weight[None]).astype(jnp.bfloat16)
+        start = num_exp * lo
+        flat_both = send_all[:, start : start + num_exp * take]
         flat_both = flat_both.reshape(num_dp * num_exp, take, 2 * slice_width)
         recv_both = lax.all_to_all(flat_both, axes, split_axis=0, concat_axis=0, tiled=True)
         recv_both = recv_both.reshape(num_exp * num_dp * take, 2 * slice_width)

time: 271 us -> 276 us (1.018)
  local copies, waits for them, and re-layouts: 35.9 us -> 40.8 us
    unnamed x32 -> x30, local copies, waits for them, and re-layouts: 4.45 us -> 6.49 us
where the time goes in v6:
time: 276 us; the launch traced here: 275 us
  waiting for transfers between devices  130 us (47%)
  starting transfers between devices  41.8 us (15%)
  matrix products  41.1 us (15%)
  local copies, waits for them, and re-layouts  40.8 us (15%)
  between operations  14.5 us (5%)
  other arithmetic  6.79 us (2%)
    ppermute x6, waiting for transfers between devices, exchange(): came = lax.ppermute(block.astype(jnp.bfloat16), 'dp', pairs)  76.7 us
    all_gather x2, waiting for transfers between devices, shards(): lax.all_gather(jnp.concatenate([grad_pre, grad_lin, activated], axis=1),...  22.7 us
    all_to_all x2, waiting for transfers between devices, shards(): lax.all_to_all(flat_both, axes, split_axis=0, concat_axis=0, tiled=True)  21.5 us
    all_to_all x2, starting transfers between devices, shards(): lax.all_to_all(flat_both, axes, split_axis=0, concat_axis=0, tiled=True)  17.6 us
    all_to_all x2, starting transfers between devices, shards(): lax.all_to_all(flat_back, axes, split_axis=0, concat_axis=0, tiled=True)  16.9 us
    dot_general x3, matrix products, contract_rows(): lax.dot_general(left, right, (((0,), (0,)), ((), ())), preferred_element_...  13.6 us
    reshape x2, local copies, waits for them, and re-layouts, shards(): recv_both = recv_both.reshape(num_exp * num_dp * take, 2 * slice_width)  9.71 us
    all_to_all x2, waiting for transfers between devices, shards(): lax.all_to_all(flat_back, axes, split_axis=0, concat_axis=0, tiled=True)  9.12 us
  transfers between devices with their start and end apart: 12, of which 7 were waited for; matrix products, arithmetic and copies ran while one was open for 26% of the time, Pallas kernels for 0%

profile of v6, /device:TPU:1, one launch (start us, length us, event | category | flops | bytes accessed | tf_op | source)
XLA Modules:
  0.0 275.0 jit_solution(16048066233384065054)
XLA Ops:
  10.5 1.1 bitcast_bitcast_fusion
  12.0 1.4 multiply_convert_fusion
  13.4 2.1 copy-done
  15.6 1.6 reshape.105
  17.3 11.9 %all-to-all-start.2 = ((bf16[128,2,3584]{2,1,0:T(2,128)(2,1)}), bf16[128,2,3584]{2,1,0:T(2,128)(2,1)}, u32[]{:S(2)}, u32[]{:S(2)}) async-start(bf16[128,2,3584]{2,1,0:T(2,128)(2,1)} %reshape.105), calls=%async_computation.2 | async-start | bytes 3670016 | tf_op jit(solution)/shard_map/all_to_all | solution.py:91
  29.2 1.8 slice-done
  31.0 4.0 %reshape.100 = bf16[128,3,3584]{2,1,0:T(4,128)(2,1)} reshape(bf16[4,96,3584]{2,1,0:T(8,128)(2,1)S(1)} %slice-done) | data formatting | bytes 5505024 | tf_op jit(solution)/shard_map/reshape | solution.py:90
  35.0 21.5 %all-to-all-done.2 = bf16[128,2,3584]{2,1,0:T(2,128)(2,1)} async-done(((bf16[128,2,3584]{2,1,0:T(2,128)(2,1)}), bf16[128,2,3584]{2,1,0:T(2,128)(2,1)}, u32[]{:S(2)}, u32[]{:S(2)}) %all-to-all-start.2) | async-done | bytes 1835040 | tf_op jit(solution)/shard_map/all_to_all | solution.py:91
  56.5 5.7 %all-to-all-start = ((bf16[128,3,3584]{2,1,0:T(4,128)(2,1)}), bf16[128,3,3584]{2,1,0:T(4,128)(2,1)}, u32[]{:S(2)}, u32[]{:S(2)}) async-start(bf16[128,3,3584]{2,1,0:T(4,128)(2,1)} %reshape.100), calls=%async_computation | async-start | bytes 7340032 | tf_op jit(solution)/shard_map/all_to_all | solution.py:91
  62.3 4.1 %reshape.106 = bf16[256,3584]{1,0:T(8,128)(2,1)S(1)} reshape(bf16[128,2,3584]{2,1,0:T(2,128)(2,1)} %all-to-all-done.2) | data formatting | bytes 3670016 | tf_op jit(solution)/shard_map/reshape | solution.py:92
  66.4 3.8 %fusion.6 = f32[256,1024]{1,0:T(8,128)S(1)} fusion(bf16[1,1792,1024]{2,1,0:T(8,128)(2,1)} %param.12, bf16[256,3584]{1,0:T(8,128)(2,1)S(1)} %reshape.106), kind=kOutput, calls=%fused_computation.11 | convolution fusion | flops 939524096 | bytes 5636096 | tf_op jit(solution)/shard_map/dot_general | solution.py:96
  70.3 1.1 fusion
  72.3 1.1 fusion.14
  73.6 1.0 fusion.61
  74.7 1.4 collective-permute-start.3
  76.0 1.3 collective-permute-start.5
  77.3 1.7 collective-permute-start.4
  79.0 33.5 %collective-permute-done.3 = bf16[64,3072]{1,0:T(8,128)(2,1)} collective-permute-done((bf16[64,3072]{1,0:T(8,128)(2,1)}, bf16[64,3072]{1,0:T(8,128)(2,1)}, u32[]{:S(2)}, u32[]{:S(2)}) %collective-permute-start.3) | collective-permute-done | bytes 393248 | tf_op jit(solution)/shard_map/ppermute | solution.py:30
  112.5 8.5 %collective-permute-done.4 = bf16[64,3072]{1,0:T(8,128)(2,1)} collective-permute-done((bf16[64,3072]{1,0:T(8,128)(2,1)S(1)}, bf16[64,3072]{1,0:T(8,128)(2,1)}, u32[]{:S(2)}, u32[]{:S(2)}) %collective-permute-start.4) | collective-permute-done | bytes 393248 | tf_op jit(solution)/shard_map/ppermute | solution.py:30
  121.0 1.4 fusion.54
  123.6 5.6 %reshape.101 = bf16[384,3584]{1,0:T(8,128)(2,1)S(1)} reshape(bf16[128,3,3584]{2,1,0:T(4,128)(2,1)} %all-to-all-done) | data formatting | bytes 5505024 | tf_op jit(solution)/shard_map/reshape | solution.py:92
  129.3 3.8 %fusion.10 = f32[384,1024]{1,0:T(8,128)S(1)} fusion(bf16[1,1792,1024]{2,1,0:T(8,128)(2,1)} %param.12, bf16[384,3584]{1,0:T(8,128)(2,1)S(1)} %reshape.101), kind=kOutput, calls=%fused_computation.15 | convolution fusion | flops 1409286144 | bytes 6619136 | tf_op jit(solution)/shard_map/dot_general | solution.py:96
  133.1 1.6 fusion.2
  135.3 1.7 fusion.18
  138.1 2.4 collective-permute-start.2
  140.5 21.8 %collective-permute-done = bf16[96,3072]{1,0:T(8,128)(2,1)S(1)} collective-permute-done((bf16[96,3072]{1,0:T(8,128)(2,1)S(1)}, bf16[96,3072]{1,0:T(8,128)(2,1)S(1)}, u32[]{:S(2)}, u32[]{:S(2)}) %collective-permute-start) | collective-permute-done | bytes 589856 | tf_op jit(solution)/shard_map/ppermute | solution.py:30
  162.3 12.9 %collective-permute-done.1 = bf16[96,3072]{1,0:T(8,128)(2,1)S(1)} collective-permute-done((bf16[96,3072]{1,0:T(8,128)(2,1)S(1)}, bf16[96,3072]{1,0:T(8,128)(2,1)S(1)}, u32[]{:S(2)}, u32[]{:S(2)}) %collective-permute-start.1) | collective-permute-done | bytes 589856 | tf_op jit(solution)/shard_map/ppermute | solution.py:30
  175.7 0.9 pad_maximum_fusion.6
  176.6 2.8 %fusion.86 = (bf16[256,1792]{1,0:T(8,128)(2,1)}, bf16[256,1792]{1,0:T(8,128)(2,1)}) fusion(bf16[256,3584]{1,0:T(8,128)(2,1)} %copy-done.1), kind=kLoop, calls=%fused_computation.113 | loop fusion | bytes 3670016 | tf_op jit(solution)/shard_map/slice | solution.py:94
  179.4 1.7 fusion.84
  181.1 3.5 %fusion.4 = f32[256,1792]{1,0:T(8,128)S(1)} fusion(bf16[1,1792,1024]{2,1,0:T(8,128)(2,1)} %param.12, bf16[256,3072]{1,0:T(8,128)(2,1)} %all-gather.5.cloned.1.call-done), kind=kOutput, calls=%fused_computation.9 | convolution fusion | flops 939524096 | bytes 6029312 | tf_op jit(solution)/shard_map/dot_general | solution.py:112
  184.6 2.2 fusion.32
  186.9 1.3 reshape.108
  188.1 8.1 %all-to-all-start.3 = ((bf16[128,2,1792]{2,1,0:T(2,128)(2,1)}), bf16[128,2,1792]{2,1,0:T(2,128)(2,1)S(1)}, u32[]{:S(2)}, u32[]{:S(2)}) async-start(bf16[128,2,1792]{2,1,0:T(2,128)(2,1)} %reshape.108), calls=%async_computation.3 | async-start | bytes 1835008 | tf_op jit(solution)/shard_map/all_to_all | solution.py:117
  196.2 22.7 %all-gather.3.cloned.1.call-done = bf16[384,3072]{1,0:T(8,128)(2,1)} async-done(((bf16[96,3072]{1,0:T(8,128)(2,1)}), bf16[384,3072]{1,0:T(8,128)(2,1)}) %all-gather.3.cloned.1.call-update) | async-done | bytes 2359312 | tf_op jit(solution)/shard_map/all_gather | solution.py:104
  218.9 4.1 %fusion.8 = f32[384,1792]{1,0:T(8,128)S(1)} fusion(bf16[1,1792,1024]{2,1,0:T(8,128)(2,1)} %param.12, bf16[384,3072]{1,0:T(8,128)(2,1)} %all-gather.3.cloned.1.call-done), kind=kOutput, calls=%fused_computation.13 | convolution fusion | flops 1409286144 | bytes 7208960 | tf_op jit(solution)/shard_map/dot_general | solution.py:112
  223.0 2.8 %fusion.26 = bf16[384,1792]{1,0:T(8,128)(2,1)S(1)} fusion(f32[384,1792]{1,0:T(8,128)S(1)} %fusion.8, bf16[1,1792,1024]{2,1,0:T(8,128)(2,1)S(1)} %copy-done.13, bf16[384,3072]{1,0:T(8,128)(2,1)} %all-gather.3.cloned.1.call-done), kind=kOutput, calls=%fused_computation.30 | convolution fusion | flops 1410662400 | bytes 8585216 | tf_op jit(solution)/shard_map/dot_general | solution.py:110
  225.8 2.1 reshape.103
  227.9 8.8 %all-to-all-start.1 = ((bf16[128,3,1792]{2,1,0:T(4,128)(2,1)}), bf16[128,3,1792]{2,1,0:T(4,128)(2,1)S(1)}, u32[]{:S(2)}, u32[]{:S(2)}) async-start(bf16[128,3,1792]{2,1,0:T(4,128)(2,1)} %reshape.103), calls=%async_computation.1 | async-start | bytes 3670016 | tf_op jit(solution)/shard_map/all_to_all | solution.py:117
  236.7 1.6 fusion.87
  238.3 1.7 copy.59
  240.2 1.1 copy-done.5
  241.6 4.5 %fusion.21 = bf16[1,1792,1024]{2,1,0:T(8,128)(2,1)} fusion(bf16[256,1792]{1,0:T(8,128)(2,1)S(1)} %copy-done.7, bf16[384,1792]{1,0:T(8,128)(2,1)S(1)} %copy-done.5, bf16[256,1024]{1,0:T(8,128)(2,1)S(1)} %get-tuple-element.18, bf16[384,1024]{1,0:T(8,128)(2,1)S(1)} %get-tuple-element.13), kind=kOutput, calls=%fused_computation.26 | convolution fusion | flops 2357854208 | bytes 7274496 | tf_op jit(solution)/shard_map/dot_general | solution.py:17
  246.1 4.5 %fusion.20 = bf16[1,1792,1024]{2,1,0:T(8,128)(2,1)} fusion(bf16[256,1792]{1,0:T(8,128)(2,1)S(1)} %copy-done.7, bf16[384,1792]{1,0:T(8,128)(2,1)S(1)} %copy-done.5, bf16[256,1024]{1,0:T(8,128)(2,1)S(1)} %get-tuple-element.19, bf16[384,1024]{1,0:T(8,128)(2,1)S(1)} %get-tuple-element.14), kind=kOutput, calls=%fused_computation.25 | convolution fusion | flops 2357854208 | bytes 7274496 | tf_op jit(solution)/shard_map/dot_general | solution.py:17
  250.6 4.5 %fusion.22 = bf16[1,1024,1792]{2,1,0:T(8,128)(2,1)} fusion(bf16[256,1792]{1,0:T(8,128)(2,1)S(1)} %copy-done.6, bf16[384,1792]{1,0:T(8,128)(2,1)S(1)} %copy-done.4, bf16[256,1024]{1,0:T(8,128)(2,1)S(1)} %get-tuple-element.17, bf16[384,1024]{1,0:T(8,128)(2,1)S(1)} %get-tuple-element.12), kind=kOutput, calls=%fused_computation.27 | convolution fusion | flops 2357854208 | bytes 7274496 | tf_op jit(solution)/shard_map/dot_general | solution.py:17
  255.2 9.1 %all-to-all-done.1 = bf16[128,3,1792]{2,1,0:T(4,128)(2,1)S(1)} async-done(((bf16[128,3,1792]{2,1,0:T(4,128)(2,1)}), bf16[128,3,1792]{2,1,0:T(4,128)(2,1)S(1)}, u32[]{:S(2)}, u32[]{:S(2)}) %all-to-all-start.1) | async-done | bytes 1376288 | tf_op jit(solution)/shard_map/all_to_all | solution.py:117
  264.3 1.3 copy.58
  265.6 1.5 pad_maximum_fusion.2
  (75 shorter events, 10.0 us)
Async XLA Ops:
  13.4 2.1 copy-start
  17.3 39.2 %all-to-all-start.2 = ((bf16[128,2,3584]{2,1,0:T(2,128)(2,1)}), bf16[128,2,3584]{2,1,0:T(2,128)(2,1)}, u32[]{:S(2)}, u32[]{:S(2)}) async-start(bf16[128,2,3584]{2,1,0:T(2,128)(2,1)} %reshape.105), calls=%async_computation.2 | async-start | bytes 3670016 | tf_op jit(solution)/shard_map/all_to_all | solution.py:91
  29.2 1.8 slice-start
  56.5 67.1 %all-to-all-start = ((bf16[128,3,3584]{2,1,0:T(4,128)(2,1)}), bf16[128,3,3584]{2,1,0:T(4,128)(2,1)}, u32[]{:S(2)}, u32[]{:S(2)}) async-start(bf16[128,3,3584]{2,1,0:T(4,128)(2,1)} %reshape.100), calls=%async_computation | async-start | bytes 7340032 | tf_op jit(solution)/shard_map/all_to_all | solution.py:91
  62.2 118.9 %all-gather.5.cloned.1.call-start = ((), (), s32[]{:S(2)}) async-start(), calls=%async_computation.5 | async-start | bytes 1966080 | tf_op jit(solution)/shard_map/all_gather | solution.py:104
  66.4 5.0 %copy-start.1 = (bf16[256,3584]{1,0:T(8,128)(2,1)}, bf16[256,3584]{1,0:T(8,128)(2,1)S(1)}, u32[]{:S(2)}) copy-start(bf16[256,3584]{1,0:T(8,128)(2,1)S(1)} %reshape.106) | copy-start | bytes 5505028
  66.4 3.9 %copy-start.8 = (bf16[1,1024,1792]{2,1,0:T(8,128)(2,1)S(1)}, bf16[1,1024,1792]{2,1,0:T(8,128)(2,1)}, u32[]{:S(2)}) copy-start(bf16[1,1024,1792]{2,1,0:T(8,128)(2,1)} %param.13) | copy-start | bytes 11010052
  70.2 2.0 copy-start.10
  74.7 37.8 %collective-permute-start.3 = (bf16[64,3072]{1,0:T(8,128)(2,1)}, bf16[64,3072]{1,0:T(8,128)(2,1)}, u32[]{:S(2)}, u32[]{:S(2)}) collective-permute-start(bf16[64,3072]{1,0:T(8,128)(2,1)} %get-tuple-element.7), channel_id=1, source_target_pairs={{0,1},{1,2},{2,3},{3,0},{4,5},{5,6},{6,7},{7,4},{8,9},{9,10},{10,1... | collective-permute-start | bytes 1179656 | tf_op jit(solution)/shard_map/ppermute | solution.py:30
  76.0 36.5 %collective-permute-start.5 = (bf16[64,3072]{1,0:T(8,128)(2,1)}, bf16[64,3072]{1,0:T(8,128)(2,1)}, u32[]{:S(2)}, u32[]{:S(2)}) collective-permute-start(bf16[64,3072]{1,0:T(8,128)(2,1)} %get-tuple-element.8), channel_id=1, source_target_pairs={{0,3},{1,0},{2,1},{3,2},{4,7},{5,4},{6,5},{7,6},{8,11},{9,8},{10,9... | collective-permute-start | bytes 1179656 | tf_op jit(solution)/shard_map/ppermute | solution.py:30
  77.3 43.7 %collective-permute-start.4 = (bf16[64,3072]{1,0:T(8,128)(2,1)S(1)}, bf16[64,3072]{1,0:T(8,128)(2,1)}, u32[]{:S(2)}, u32[]{:S(2)}) collective-permute-start(bf16[64,3072]{1,0:T(8,128)(2,1)S(1)} %get-tuple-element.9), channel_id=1, source_target_pairs={{0,2},{1,3},{2,0},{3,1},{4,6},{5,7},{6,4},{7,5},{8,10},{9,11},{10,... | collective-permute-start | bytes 1179656 | tf_op jit(solution)/shard_map/ppermute | solution.py:30
  123.4 95.5 %all-gather.3.cloned.1.call-start = ((), (), s32[]{:S(2)}) async-start(), calls=%async_computation.4 | async-start | bytes 2949120 | tf_op jit(solution)/shard_map/all_gather | solution.py:104
  129.3 3.8 %copy-start.9 = (bf16[1,1024,1792]{2,1,0:T(8,128)(2,1)S(1)}, bf16[1,1024,1792]{2,1,0:T(8,128)(2,1)}, u32[]{:S(2)}) copy-start(bf16[1,1024,1792]{2,1,0:T(8,128)(2,1)} %param.13) | copy-start | bytes 11010052
  133.1 2.2 copy-start.11
  137.7 24.5 %collective-permute-start = (bf16[96,3072]{1,0:T(8,128)(2,1)S(1)}, bf16[96,3072]{1,0:T(8,128)(2,1)S(1)}, u32[]{:S(2)}, u32[]{:S(2)}) collective-permute-start(bf16[96,3072]{1,0:T(8,128)(2,1)S(1)} %get-tuple-element.4), channel_id=1, source_target_pairs={{0,1},{1,2},{2,3},{3,0},{4,5},{5,6},{6,7},{7,4},{8,9},{9,10},{10,1... | collective-permute-start | bytes 1769480 | tf_op jit(solution)/shard_map/ppermute | solution.py:30
  138.1 24.1 %collective-permute-start.2 = (bf16[96,3072]{1,0:T(8,128)(2,1)S(1)}, bf16[96,3072]{1,0:T(8,128)(2,1)S(1)}, u32[]{:S(2)}, u32[]{:S(2)}) collective-permute-start(bf16[96,3072]{1,0:T(8,128)(2,1)S(1)} %get-tuple-element.5), channel_id=1, source_target_pairs={{0,3},{1,0},{2,1},{3,2},{4,7},{5,4},{6,5},{7,6},{8,11},{9,8},{10,9... | collective-permute-start | bytes 1769480 | tf_op jit(solution)/shard_map/ppermute | solution.py:30
  140.5 34.7 %collective-permute-start.1 = (bf16[96,3072]{1,0:T(8,128)(2,1)S(1)}, bf16[96,3072]{1,0:T(8,128)(2,1)S(1)}, u32[]{:S(2)}, u32[]{:S(2)}) collective-permute-start(bf16[96,3072]{1,0:T(8,128)(2,1)S(1)} %get-tuple-element.6), channel_id=1, source_target_pairs={{0,2},{1,3},{2,0},{3,1},{4,6},{5,7},{6,4},{7,5},{8,10},{9,11},{10,... | collective-permute-start | bytes 1769480 | tf_op jit(solution)/shard_map/ppermute | solution.py:30
  181.1 3.5 %copy-start.12 = (bf16[1,1792,1024]{2,1,0:T(8,128)(2,1)S(1)}, bf16[1,1792,1024]{2,1,0:T(8,128)(2,1)}, u32[]{:S(2)}) copy-start(bf16[1,1792,1024]{2,1,0:T(8,128)(2,1)} %param.11) | copy-start | bytes 11010052
  188.1 39.7 %all-to-all-start.3 = ((bf16[128,2,1792]{2,1,0:T(2,128)(2,1)}), bf16[128,2,1792]{2,1,0:T(2,128)(2,1)S(1)}, u32[]{:S(2)}, u32[]{:S(2)}) async-start(bf16[128,2,1792]{2,1,0:T(2,128)(2,1)} %reshape.108), calls=%async_computation.3 | async-start | bytes 1835008 | tf_op jit(solution)/shard_map/all_to_all | solution.py:117
  218.9 4.1 %copy-start.13 = (bf16[1,1792,1024]{2,1,0:T(8,128)(2,1)S(1)}, bf16[1,1792,1024]{2,1,0:T(8,128)(2,1)}, u32[]{:S(2)}) copy-start(bf16[1,1792,1024]{2,1,0:T(8,128)(2,1)} %param.11) | copy-start | bytes 11010052
  227.9 36.4 %all-to-all-start.1 = ((bf16[128,3,1792]{2,1,0:T(4,128)(2,1)}), bf16[128,3,1792]{2,1,0:T(4,128)(2,1)S(1)}, u32[]{:S(2)}, u32[]{:S(2)}) async-start(bf16[128,3,1792]{2,1,0:T(4,128)(2,1)} %reshape.103), calls=%async_computation.1 | async-start | bytes 3670016 | tf_op jit(solution)/shard_map/all_to_all | solution.py:117
  236.7 3.3 %copy-start.3 = (bf16[384,3072]{1,0:T(8,128)(2,1)S(1)}, bf16[384,3072]{1,0:T(8,128)(2,1)}, u32[]{:S(2)}) copy-start(bf16[384,3072]{1,0:T(8,128)(2,1)} %all-gather.3.cloned.1.call-done) | copy-start | bytes 7077892
  240.0 1.3 copy-start.5
  240.0 1.6 copy-start.7
  246.1 4.5 %copy-start.4 = (bf16[384,1792]{1,0:T(8,128)(2,1)S(1)}, bf16[384,1792]{1,0:T(8,128)(2,1)}, u32[]{:S(2)}) copy-start(bf16[384,1792]{1,0:T(8,128)(2,1)} %get-tuple-element.10) | copy-start | bytes 4128772
  246.1 4.5 %copy-start.6 = (bf16[256,1792]{1,0:T(8,128)(2,1)S(1)}, bf16[256,1792]{1,0:T(8,128)(2,1)}, u32[]{:S(2)}) copy-start(bf16[256,1792]{1,0:T(8,128)(2,1)} %get-tuple-element.15) | copy-start | bytes 2752516
  255.1 10.4 %copy-start.2 = (bf16[4,32,2,1792]{3,0,2,1:T(4,128)(2,1)S(1)}, bf16[4,32,2,1792]{3,0,2,1:T(4,128)(2,1)}, u32[]{:S(2)}) copy-start(bf16[4,32,2,1792]{3,0,2,1:T(4,128)(2,1)} %copy.59) | copy-start | bytes 2752516
Sparse Core Ops, SparseCore 0:
  123.5 33.8 all-gather.4
  176.7 42.1 all-gather.2
